TPU v7x, 128 devices: a whole 4x4x4 slice. The times are simulated.
128 devices in a mesh: gx: 32 (over y, x, core), gy: 4 (over z).
Axes of the slice: x: 4, y: 4, z: 4, core: 2. Of those that a mesh axis runs over, the one named last changes fastest.
Arguments:
- east_blocks: int32 [64, 4], P(None, 'gy'), may hold values from 0 to 2, as said below
- job_code: int32 [832, 4], P('gx', 'gy'), may hold values from -1 to 2282, as said below
- factor_panels: bfloat16 [832, 4, 2, 1536, 128], P('gx', 'gy'), as said below
- dual_rhs: float32 [64, 4, 256, 384], P('gx', 'gy'), may hold values from -6 to 6
Outputs:
- multipliers: float32 [64, 4, 256, 384], P('gx', 'gy')
- residual: float32 [64, 4, 256, 384], P('gx', 'gy')
Inputs may be any that keep to these rules, and one draw needn't show every extreme that they name: `east_blocks`: in each row sy the faces sx = s0 to s0 + 15 carry 2 blocks, for a start s0 drawn per row from 1 to 46; the other faces carry 1, and the face at sx = 63 carries 0. `job_code`: A code (sx * 6 + bi) * 6 + bj names the upper tile bi <= bj < nb of subdomain (sx, sy) for column sy. In each column the live tiles, ordered by sx, then bi, then bj, are numbered k = 0, 1, ... and sit at row (k % 32) * 26 + k // 32; all other slots hold -1. Hence one device of gx forms at most 2 tiles of the subdomains of one gx index, and exactly 2 for some. `factor_panels`: A live slot holds column blocks bi and bj of subdomain (sx, sy)'s factor of 1536 rows and 768 columns, the same block wherever it appears; empty slots hold zeros.
All inputs are finite; a program needn't handle non-finite values.
Results may differ from a plain program's by a relative error of at most 0.0059.
Values may be sent and summed in bfloat16 or wider, within the bound.
No kernel may reach another device: no remote copies, remote signals or barrier semaphores. Data moves between devices by JAX's collectives and lax.ppermute only.
A program may use at most 128 MiB of HBM per device.

v0:
```python
from functools import partial

import jax
import jax.numpy as jnp
from jax import lax
from jax.experimental import pallas as pl
from jax.experimental.pallas import tpu as pltpu
from jax.sharding import PartitionSpec as P

NB = 6
ITERS = 4


CHEB_LOW = 0.2
CHEB_HIGH = 7.0


def from_behind(value, axis, steps):
    count = lax.axis_size(axis)
    initial, last = (max(0, -steps), min(count, count - steps))
    return lax.ppermute(value, axis, [(source, source + steps) for source in range(initial, last)])


def _pack_kernel(table_ref, tiles_ref, out_ref, *, rows, block_len):
    for r in range(rows):
        tile = tiles_ref[table_ref[0, r]]
        keep = table_ref[1, r] != 0
        out_ref[r * block_len : (r + 1) * block_len, :] = jnp.where(keep, tile, jnp.zeros_like(tile))


def pack_tiles(table, tiles, rows):
    block_len = tiles.shape[-1]
    size = 2 * block_len * block_len
    return pl.pallas_call(
        partial(_pack_kernel, rows=rows, block_len=block_len),
        out_shape=jax.ShapeDtypeStruct((rows * block_len, block_len), tiles.dtype),
        in_specs=[
            pl.BlockSpec(memory_space=pltpu.SMEM),
            pl.BlockSpec(memory_space=pltpu.VMEM),
        ],
        out_specs=pl.BlockSpec(memory_space=pltpu.VMEM),
        cost_estimate=pl.CostEstimate(
            flops=0, transcendentals=0, bytes_accessed=(tiles.shape[0] + rows) * size
        ),
    )(table, tiles)


def _matrix_kernel(table_ref, tiles_ref, out_ref, *, subs, blocks, block_len):
    for s in range(subs):
        for p in range(blocks):
            for q in range(p, blocks):
                entry = (s * blocks + p) * blocks + q
                tile = tiles_ref[table_ref[0, entry]]
                keep = table_ref[1, entry] != 0
                tile = jnp.where(keep, tile, jnp.zeros_like(tile))
                out_ref[s, p * block_len : (p + 1) * block_len, q * block_len : (q + 1) * block_len] = tile
                if q > p:
                    out_ref[s, q * block_len : (q + 1) * block_len, p * block_len : (p + 1) * block_len] = (
                        tile.astype(jnp.float32).T.astype(tile.dtype)
                    )


def matrix_tiles(table, tiles, subs, blocks):
    block_len = tiles.shape[-1]
    size = 2 * block_len * block_len
    width = blocks * block_len
    return pl.pallas_call(
        partial(_matrix_kernel, subs=subs, blocks=blocks, block_len=block_len),
        out_shape=jax.ShapeDtypeStruct((subs, width, width), tiles.dtype),
        in_specs=[
            pl.BlockSpec(memory_space=pltpu.SMEM),
            pl.BlockSpec(memory_space=pltpu.VMEM),
        ],
        out_specs=pl.BlockSpec(memory_space=pltpu.VMEM),
        cost_estimate=pl.CostEstimate(
            flops=0, transcendentals=0, bytes_accessed=(tiles.shape[0] + subs * blocks * blocks) * size
        ),
    )(table, tiles)


def face_mask(counts, block_len):
    east_lane = jnp.arange(2 * block_len, dtype=jnp.int32) // block_len
    east_ok = east_lane < counts[..., 1:2]
    north_ok = jnp.zeros((block_len,), jnp.int32) < counts[..., 3:4]
    return jnp.concatenate([east_ok, north_ok], axis=-1).astype(jnp.float32)


def logical_slots(counts):
    west_n = counts[:, 0:1]
    east_n = counts[:, 1:2]
    south_n = counts[:, 2:3]
    north_n = counts[:, 3:4]
    within = jnp.array([0, 1, 0, 1, 0, 0], jnp.int32)[None, :]
    zero = jnp.zeros_like(west_n)
    offsets = jnp.concatenate(
        [zero, zero, west_n, west_n, west_n + east_n, west_n + east_n + south_n], axis=1
    )
    limits = jnp.concatenate([west_n, west_n, east_n, east_n, south_n, north_n], axis=1)
    return offsets + within, within < limits


def shards(east_blocks, job_code, factor_panels, dual_rhs):
    gx_count = lax.axis_size("gx")
    gy_count = lax.axis_size("gy")
    gx_index = lax.axis_index("gx")
    gy_index = lax.axis_index("gy")
    block_len = factor_panels.shape[-1]
    sub_count = dual_rhs.shape[0]
    column = east_blocks[:, 0]
    west_column = jnp.concatenate([jnp.zeros((1,), jnp.int32), column[:-1]])
    south_one = (gy_index > 0).astype(jnp.int32)
    north_one = (gy_index < gy_count - 1).astype(jnp.int32)
    blocks_all = west_column + column + south_one + north_one
    tiles_all = blocks_all * (blocks_all + 1) // 2
    first_tile_all = jnp.cumsum(tiles_all) - tiles_all
    first_sub = gx_index * sub_count
    east_own = lax.dynamic_slice_in_dim(column, first_sub, sub_count)
    west_own = lax.dynamic_slice_in_dim(west_column, first_sub, sub_count)
    blocks_own = lax.dynamic_slice_in_dim(blocks_all, first_sub, sub_count)
    first_tile_own = lax.dynamic_slice_in_dim(first_tile_all, first_sub, sub_count)
    south_own = jnp.broadcast_to(south_one, (sub_count,))
    north_own = jnp.broadcast_to(north_one, (sub_count,))
    counts = jnp.stack([west_own, east_own, south_own, north_own], axis=-1)

    residual = dual_rhs[:, 0] * face_mask(counts, block_len)[:, None, :]
    west_residual = from_behind(residual[sub_count - 1, :, : 2 * block_len], "gx", 1)
    south_residual = from_behind(residual[..., 2 * block_len :], "gy", 1)

    tiles = jnp.einsum(
        "jka,jkb->jab",
        factor_panels[:, 0, 0],
        factor_panels[:, 0, 1],
        preferred_element_type=jnp.float32,
    ).astype(jnp.bfloat16)
    tile_codes = job_code[:, 0]
    job_count = tile_codes.shape[0]
    is_valid = tile_codes >= 0
    owner_gx = jnp.where(is_valid, tile_codes // (NB * NB) // sub_count, 0)
    slot_cap = (sub_count * NB * (NB + 1) // 2 + gx_count - 1) // gx_count
    job_order = jnp.arange(job_count, dtype=jnp.int32)
    same_owner = (
        (owner_gx[:, None] == owner_gx[None, :])
        & is_valid[None, :]
        & (job_order[None, :] < job_order[:, None])
    )
    slot_rank = jnp.sum(same_owner.astype(jnp.int32), axis=1)
    send_slot = jnp.where(is_valid & (slot_rank < slot_cap), owner_gx * slot_cap + slot_rank, -1)
    slot_count = gx_count * slot_cap
    send_hit = send_slot[None, :] == jnp.arange(slot_count, dtype=jnp.int32)[:, None]
    send_from = jnp.sum(jnp.where(send_hit, job_order[None, :], 0), axis=1)
    send_mode = jnp.any(send_hit, axis=1).astype(jnp.int32)
    send_tiles = pack_tiles(jnp.stack([send_from, send_mode]), tiles, slot_count)
    send_tiles = send_tiles.reshape(gx_count, slot_cap * block_len, block_len)
    got_tiles = lax.all_to_all(send_tiles, "gx", split_axis=0, concat_axis=0, tiled=True)
    got_tiles = got_tiles.reshape(slot_count, block_len, block_len)

    source, alive = logical_slots(counts)
    row_slot = source[:, :, None]
    col_slot = source[:, None, :]
    low_slot = jnp.minimum(row_slot, col_slot)
    high_slot = jnp.maximum(row_slot, col_slot)
    nb = blocks_own[:, None, None]
    pair_index = low_slot * nb - low_slot * (low_slot - 1) // 2 + (high_slot - low_slot)
    tile_number = first_tile_own[:, None, None] + pair_index
    local_number = tile_number - first_tile_own[0]
    got_slot = tile_number % gx_count * slot_cap + local_number // gx_count
    both_alive = alive[:, :, None] & alive[:, None, :]
    matrix_mode = both_alive.astype(jnp.int32)
    matrix_from = jnp.where(both_alive, jnp.clip(got_slot, 0, slot_count - 1), 0)
    matrices = matrix_tiles(
        jnp.stack([matrix_from.reshape(-1), matrix_mode.reshape(-1)]), got_tiles, sub_count, NB
    )

    cases = residual.shape[1]
    cheb_center = (CHEB_HIGH + CHEB_LOW) / 2.0
    cheb_radius = (CHEB_HIGH - CHEB_LOW) / 2.0
    cheb_ratio = cheb_center / cheb_radius
    cheb_rho = 1.0 / cheb_ratio
    update = residual / cheb_center
    west_update = west_residual / cheb_center
    south_update = south_residual / cheb_center
    multipliers = jnp.zeros_like(residual)
    for sweep in range(ITERS):
        multipliers = multipliers + update
        east_part = update[..., : 2 * block_len]
        to_north_part = update[..., 2 * block_len :]
        west_in = -jnp.concatenate([west_update[None], east_part[: sub_count - 1]], axis=0)
        local_vec = jnp.concatenate([west_in, east_part, -south_update, to_north_part], axis=-1)
        high_f = lax.reduce_precision(local_vec, exponent_bits=8, mantissa_bits=7)
        high = high_f.astype(jnp.bfloat16)
        low = (local_vec - high_f).astype(jnp.bfloat16)
        both = jnp.einsum(
            "ncm,nmk->nck",
            jnp.concatenate([high, low], axis=1),
            matrices,
            preferred_element_type=jnp.float32,
        )
        image = both[:, :cases] + both[:, cases:]
        west_part = image[..., : 2 * block_len]
        split_east_part = image[..., 2 * block_len : 4 * block_len]
        south_part = image[..., 4 * block_len : 5 * block_len]
        split_north_part = image[..., 5 * block_len :]
        from_east = from_behind(west_part[0], "gx", -1)
        from_north = from_behind(south_part, "gy", -1)
        last = sweep == ITERS - 1
        if not last:
            west_east_part = from_behind(split_east_part[sub_count - 1], "gx", 1)
            south_north_part = from_behind(split_north_part, "gy", 1)
        east_near = jnp.concatenate([west_part[1:], from_east[None]], axis=0)
        residual = residual - jnp.concatenate(
            [split_east_part - east_near, split_north_part - from_north], axis=-1
        )
        rho_next = 1.0 / (2.0 * cheb_ratio - cheb_rho)
        keep = rho_next * cheb_rho
        step = 2.0 * rho_next / cheb_radius
        update = keep * update + step * residual
        if not last:
            west_residual = west_residual - (west_east_part - west_part[0])
            south_residual = south_residual - (south_north_part - south_part)
            west_update = keep * west_update + step * west_residual
            south_update = keep * south_update + step * south_residual
        cheb_rho = rho_next
    return (multipliers[:, None], residual[:, None])


def solution(mesh):
    in_specs = (
        P(None, "gy"),
        P("gx", "gy"),
        P("gx", "gy", None, None, None),
        P("gx", "gy", None, None),
    )
    out_specs = (P("gx", "gy", None, None), P("gx", "gy", None, None))
    return jax.shard_map(shards, mesh=mesh, in_specs=in_specs, out_specs=out_specs, check_vma=False)
```

profile of v0, /device:TPU:17, one launch (start us, length us, event | category | flops | bytes accessed | tf_op | source)
XLA Modules:
  0.0 140.1 jit_solution(8463801500975568669)
XLA Ops:
  3.7 9.5 %fusion.25.tiles_ref = bf16[26,128,128]{2,1,0:T(8,128)(2,1)} fusion(bf16[26,1,2,1536,128]{4,3,2,1,0:T(8,128)(2,1)} %param.7), kind=kOutput, calls=%fused_computation.41 | convolution fusion | flops 1309048832 | bytes 21299200 | tf_op jit(solution)/shard_map/jka,jkb->jab/dot_general | solution.py:129
  13.8 3.0 %shard_map.68 = bf16[8192,128]{1,0:T(8,128)(2,1)} custom-call(s32[2,64]{1,0:T(2,128)} %pad_add_fusion.1.table_ref, bf16[26,128,128]{2,1,0:T(8,128)(2,1)} %fusion.25.tiles_ref), custom_call_target="tpu_custom_call" | custom-call | bytes 2949120 | tf_op jit(solution)/shard_map/pallas_call | solution.py:34
  16.8 7.8 %all-to-all-start = ((bf16[32,256,128]{2,1,0:T(8,128)(2,1)}), bf16[32,256,128]{2,1,0:T(8,128)(2,1)S(1)}, u32[]{:S(2)}, u32[]{:S(2)}) async-start(bf16[32,256,128]{2,1,0:T(8,128)(2,1)} %bitcast.137), calls=%async_computation | async-start | bytes 4194304 | tf_op jit(solution)/shard_map/all_to_all | solution.py:154
  25.3 2.1 %broadcast_multiply_fusion = (f32[2,256,384]{2,1,0:T(8,128)}, f32[2,256,384]{2,1,0:T(8,128)S(1)}) fusion(f32[2,384]{1,0:T(2,128)S(1)} %pad_convert_fusion, f32[2,1,256,384]{3,2,1,0:T(8,128)} %param.8), kind=kLoop, calls=%fused_computation.66 | loop fusion | flops 393216 | bytes 2362368 | tf_op jit(solution)/shard_map/div | solution.py:179
  28.2 3.4 %collective-permute-start = (f32[256,256]{1,0:T(8,128)}, f32[256,256]{1,0:T(8,128)S(1)}, u32[]{:S(2)}, u32[]{:S(2)}) collective-permute-start(f32[256,256]{1,0:T(8,128)} %slice_bitcast_fusion.7), channel_id=1, source_target_pairs={{0,4},{4,8},{8,12},{12,16},{16,20},{20,24},{24,28},{28,32},{32,36}... | collective-permute-start | bytes 786440 | tf_op jit(solution)/shard_map/ppermute | solution.py:21
  32.3 3.5 %collective-permute-start.1 = (f32[2,256,128]{2,1,0:T(8,128)}, f32[2,256,128]{2,1,0:T(8,128)S(1)}, u32[]{:S(2)}, u32[]{:S(2)}) collective-permute-start(f32[2,256,128]{2,1,0:T(8,128)} %slice.225), channel_id=1, source_target_pairs={{0,1},{1,2},{2,3},{4,5},{5,6},{6,7},{8,9},{9,10},{10,11},{12,13},{... | collective-permute-start | bytes 786440 | tf_op jit(solution)/shard_map/ppermute | solution.py:21
  35.9 1.7 %slice.226 = f32[2,256,128]{2,1,0:T(8,128)} slice(f32[2,256,384]{2,1,0:T(8,128)} %get-tuple-element.16), slice={[0:2], [0:256], [256:384]} | slice | bytes 524288 | tf_op jit(solution)/shard_map/slice | solution.py:186
  37.6 1.7 %slice.223 = f32[1,256,256]{2,1,0:T(8,128)} slice(f32[2,256,384]{2,1,0:T(8,128)} %get-tuple-element.16), slice={[0:1], [0:256], [0:256]} | slice | bytes 524288 | tf_op jit(solution)/shard_map/slice | solution.py:187
  39.3 1.9 %slice.224 = f32[2,256,256]{2,1,0:T(8,128)} slice(f32[2,256,384]{2,1,0:T(8,128)} %get-tuple-element.16), slice={[0:2], [0:256], [0:256]} | slice | bytes 1048576 | tf_op jit(solution)/shard_map/slice | solution.py:185
  43.2 8.4 %collective-permute-done = f32[256,256]{1,0:T(8,128)S(1)} collective-permute-done((f32[256,256]{1,0:T(8,128)}, f32[256,256]{1,0:T(8,128)S(1)}, u32[]{:S(2)}, u32[]{:S(2)}) %collective-permute-start) | collective-permute-done | bytes 262176 | tf_op jit(solution)/shard_map/ppermute | solution.py:21
  55.4 3.5 %shard_map.69 = bf16[2,768,768]{2,1,0:T(8,128)(2,1)} custom-call(s32[2,72]{1,0:T(2,128)} %pad_add_fusion.table_ref, bf16[64,128,128]{2,1,0:T(8,128)(2,1)} %bitcast.136), custom_call_target="tpu_custom_call" | custom-call | bytes 4456448 | tf_op jit(solution)/shard_map/pallas_call | solution.py:67
  58.8 3.5 %fusion.9 = f32[2,512,768]{2,1,0:T(8,128)S(1)} fusion(bf16[2,768,768]{2,1,0:T(8,128)(2,1)} %shard_map.69, bf16[2,256,768]{2,1,0:T(8,128)(2,1)} %get-tuple-element.54, bf16[2,256,768]{2,1,0:T(8,128)(2,1)} %get-tuple-element.53), kind=kOutput, calls=%fused_computation.22 | convolution fusion | flops 1211105280 | bytes 7077888 | tf_op jit(solution)/shard_map/ncm,nmk->nck/dot_general | solution.py:192
  62.6 4.4 %collective-permute-start.2 = (f32[256,256]{1,0:T(8,128)S(1)}, f32[256,256]{1,0:T(8,128)S(1)}, u32[]{:S(2)}, u32[]{:S(2)}) collective-permute-start(f32[256,256]{1,0:T(8,128)S(1)} %get-tuple-element.48), channel_id=1, source_target_pairs={{4,0},{8,4},{12,8},{16,12},{20,16},{24,20},{28,24},{32,28},{36,32}... | collective-permute-start | bytes 786440 | tf_op jit(solution)/shard_map/ppermute | solution.py:21
  67.1 3.6 %collective-permute-start.5 = (f32[2,256,128]{2,1,0:T(8,128)S(1)}, f32[2,256,128]{2,1,0:T(8,128)S(1)}, u32[]{:S(2)}, u32[]{:S(2)}) collective-permute-start(f32[2,256,128]{2,1,0:T(8,128)S(1)} %get-tuple-element.51), channel_id=1, source_target_pairs={{0,1},{1,2},{2,3},{4,5},{5,6},{6,7},{8,9},{9,10},{10,11},{12,13},{... | collective-permute-start | bytes 786440 | tf_op jit(solution)/shard_map/ppermute | solution.py:21
  71.9 2.1 %collective-permute-start.4 = (f32[256,256]{1,0:T(8,128)S(1)}, f32[256,256]{1,0:T(8,128)S(1)}, u32[]{:S(2)}, u32[]{:S(2)}) collective-permute-start(f32[256,256]{1,0:T(8,128)S(1)} %get-tuple-element.47), channel_id=1, source_target_pairs={{0,4},{4,8},{8,12},{12,16},{16,20},{20,24},{24,28},{28,32},{32,36}... | collective-permute-start | bytes 786440 | tf_op jit(solution)/shard_map/ppermute | solution.py:21
  74.1 2.1 %collective-permute-done.5 = f32[2,256,128]{2,1,0:T(8,128)S(1)} collective-permute-done((f32[2,256,128]{2,1,0:T(8,128)S(1)}, f32[2,256,128]{2,1,0:T(8,128)S(1)}, u32[]{:S(2)}, u32[]{:S(2)}) %collective-permute-start.5) | collective-permute-done | bytes 262176 | tf_op jit(solution)/shard_map/ppermute | solution.py:21
  76.2 4.2 %collective-permute-done.3 = f32[2,256,128]{2,1,0:T(8,128)S(1)} collective-permute-done((f32[2,256,128]{2,1,0:T(8,128)S(1)}, f32[2,256,128]{2,1,0:T(8,128)S(1)}, u32[]{:S(2)}, u32[]{:S(2)}) %collective-permute-start.3) | collective-permute-done | bytes 262176 | tf_op jit(solution)/shard_map/ppermute | solution.py:21
  81.2 1.4 %copy-done.2 = bf16[2,768,768]{2,1,0:T(8,128)(2,1)S(1)} copy-done((bf16[2,768,768]{2,1,0:T(8,128)(2,1)S(1)}, bf16[2,768,768]{2,1,0:T(8,128)(2,1)}, u32[]{:S(2)}) %copy-start.2) | copy-done | bytes 2359320
  84.2 3.1 %collective-permute-start.6 = (f32[256,256]{1,0:T(8,128)S(1)}, f32[256,256]{1,0:T(8,128)S(1)}, u32[]{:S(2)}, u32[]{:S(2)}) collective-permute-start(f32[256,256]{1,0:T(8,128)S(1)} %get-tuple-element.40), channel_id=1, source_target_pairs={{4,0},{8,4},{12,8},{16,12},{20,16},{24,20},{28,24},{32,28},{36,32}... | collective-permute-start | bytes 786440 | tf_op jit(solution)/shard_map/ppermute | solution.py:21
  87.4 4.3 %collective-permute-start.9 = (f32[2,256,128]{2,1,0:T(8,128)S(1)}, f32[2,256,128]{2,1,0:T(8,128)S(1)}, u32[]{:S(2)}, u32[]{:S(2)}) collective-permute-start(f32[2,256,128]{2,1,0:T(8,128)S(1)} %get-tuple-element.43), channel_id=1, source_target_pairs={{0,1},{1,2},{2,3},{4,5},{5,6},{6,7},{8,9},{9,10},{10,11},{12,13},{... | collective-permute-start | bytes 786440 | tf_op jit(solution)/shard_map/ppermute | solution.py:21
  93.0 1.9 %collective-permute-start.8 = (f32[256,256]{1,0:T(8,128)S(1)}, f32[256,256]{1,0:T(8,128)S(1)}, u32[]{:S(2)}, u32[]{:S(2)}) collective-permute-start(f32[256,256]{1,0:T(8,128)S(1)} %get-tuple-element.39), channel_id=1, source_target_pairs={{0,4},{4,8},{8,12},{12,16},{16,20},{20,24},{24,28},{28,32},{32,36}... | collective-permute-start | bytes 786440 | tf_op jit(solution)/shard_map/ppermute | solution.py:21
  95.0 1.7 %collective-permute-done.9 = f32[2,256,128]{2,1,0:T(8,128)S(1)} collective-permute-done((f32[2,256,128]{2,1,0:T(8,128)S(1)}, f32[2,256,128]{2,1,0:T(8,128)S(1)}, u32[]{:S(2)}, u32[]{:S(2)}) %collective-permute-start.9) | collective-permute-done | bytes 262176 | tf_op jit(solution)/shard_map/ppermute | solution.py:21
  96.7 4.2 %collective-permute-done.7 = f32[2,256,128]{2,1,0:T(8,128)S(1)} collective-permute-done((f32[2,256,128]{2,1,0:T(8,128)S(1)}, f32[2,256,128]{2,1,0:T(8,128)S(1)}, u32[]{:S(2)}, u32[]{:S(2)}) %collective-permute-start.7) | collective-permute-done | bytes 262176 | tf_op jit(solution)/shard_map/ppermute | solution.py:21
  103.5 4.1 %collective-permute-start.10 = (f32[256,256]{1,0:T(8,128)S(1)}, f32[256,256]{1,0:T(8,128)S(1)}, u32[]{:S(2)}, u32[]{:S(2)}) collective-permute-start(f32[256,256]{1,0:T(8,128)S(1)} %get-tuple-element.31), channel_id=1, source_target_pairs={{4,0},{8,4},{12,8},{16,12},{20,16},{24,20},{28,24},{32,28},{36,32}... | collective-permute-start | bytes 786440 | tf_op jit(solution)/shard_map/ppermute | solution.py:21
  107.7 4.3 %collective-permute-start.13 = (f32[2,256,128]{2,1,0:T(8,128)S(1)}, f32[2,256,128]{2,1,0:T(8,128)S(1)}, u32[]{:S(2)}, u32[]{:S(2)}) collective-permute-start(f32[2,256,128]{2,1,0:T(8,128)S(1)} %get-tuple-element.35), channel_id=1, source_target_pairs={{0,1},{1,2},{2,3},{4,5},{5,6},{6,7},{8,9},{9,10},{10,11},{12,13},{... | collective-permute-start | bytes 786440 | tf_op jit(solution)/shard_map/ppermute | solution.py:21
  113.4 2.1 %collective-permute-start.12 = (f32[256,256]{1,0:T(8,128)S(1)}, f32[256,256]{1,0:T(8,128)S(1)}, u32[]{:S(2)}, u32[]{:S(2)}) collective-permute-start(f32[256,256]{1,0:T(8,128)S(1)} %get-tuple-element.30), channel_id=1, source_target_pairs={{0,4},{4,8},{8,12},{12,16},{16,20},{20,24},{24,28},{28,32},{32,36}... | collective-permute-start | bytes 786440 | tf_op jit(solution)/shard_map/ppermute | solution.py:21
  115.6 2.0 %collective-permute-done.13 = f32[2,256,128]{2,1,0:T(8,128)S(1)} collective-permute-done((f32[2,256,128]{2,1,0:T(8,128)S(1)}, f32[2,256,128]{2,1,0:T(8,128)S(1)}, u32[]{:S(2)}, u32[]{:S(2)}) %collective-permute-start.13) | collective-permute-done | bytes 262176 | tf_op jit(solution)/shard_map/ppermute | solution.py:21
  117.6 3.8 %collective-permute-done.11 = f32[2,256,128]{2,1,0:T(8,128)S(1)} collective-permute-done((f32[2,256,128]{2,1,0:T(8,128)S(1)}, f32[2,256,128]{2,1,0:T(8,128)S(1)}, u32[]{:S(2)}, u32[]{:S(2)}) %collective-permute-start.11) | collective-permute-done | bytes 262176 | tf_op jit(solution)/shard_map/ppermute | solution.py:21
  124.0 3.3 %collective-permute-start.14 = (f32[256,256]{1,0:T(8,128)S(1)}, f32[256,256]{1,0:T(8,128)S(1)}, u32[]{:S(2)}, u32[]{:S(2)}) collective-permute-start(f32[256,256]{1,0:T(8,128)S(1)} %get-tuple-element.27), channel_id=1, source_target_pairs={{4,0},{8,4},{12,8},{16,12},{20,16},{24,20},{28,24},{32,28},{36,32}... | collective-permute-start | bytes 786440 | tf_op jit(solution)/shard_map/ppermute | solution.py:21
  128.9 2.8 %collective-permute-done.14 = f32[256,256]{1,0:T(8,128)S(1)} collective-permute-done((f32[256,256]{1,0:T(8,128)S(1)}, f32[256,256]{1,0:T(8,128)S(1)}, u32[]{:S(2)}, u32[]{:S(2)}) %collective-permute-start.14) | collective-permute-done | bytes 262176 | tf_op jit(solution)/shard_map/ppermute | solution.py:21
  131.8 6.6 %collective-permute-done.15 = f32[2,256,128]{2,1,0:T(8,128)S(1)} collective-permute-done((f32[2,256,128]{2,1,0:T(8,128)S(1)}, f32[2,256,128]{2,1,0:T(8,128)S(1)}, u32[]{:S(2)}, u32[]{:S(2)}) %collective-permute-start.15) | collective-permute-done | bytes 262176 | tf_op jit(solution)/shard_map/ppermute | solution.py:21
  138.5 1.6 %fusion.32 = (f32[2,1,256,384]{3,2,1,0:T(8,128)}, f32[2,1,256,384]{3,2,1,0:T(8,128)}) fusion(f32[2,1,256,128]{3,2,0,1:T(8,128)S(1)} %fusion.34, f32[2,1,256,256]{3,2,0,1:T(8,128)S(1)} %fusion.33, f32[2,1,256,128]{3,2,0,1:T(8,128)S(1)} %bitcast.141, f32[2,1,256,256]{3,2,0,1:T(8,128)S(1)} %fusion.65, f32[2,1,256,128]{3,2,0,1:T(8,128)S(1)} %bitcast.140, ...), kind=kLoop, calls=%fused_computation.51 | loop fusion | flops 4325376 | bytes 5508096
  (122 shorter events, 25.2 us)
Async XLA Ops:
  16.8 7.9 %copy-start.5 = (s32[64,1]{0,1:T(1,128)S(1)}, s32[64,1]{0,1:T(1,128)}, u32[]{:S(2)}) copy-start(s32[64,1]{0,1:T(1,128)} %param.5) | copy-start | bytes 772
  16.8 37.2 %all-to-all-start = ((bf16[32,256,128]{2,1,0:T(8,128)(2,1)}), bf16[32,256,128]{2,1,0:T(8,128)(2,1)S(1)}, u32[]{:S(2)}, u32[]{:S(2)}) async-start(bf16[32,256,128]{2,1,0:T(8,128)(2,1)} %bitcast.137), calls=%async_computation | async-start | bytes 4194304 | tf_op jit(solution)/shard_map/all_to_all | solution.py:154
  27.5 14.2 %copy-start.6 = (s32[6]{0:T(128)S(1)}, s32[6]{0:T(128)}, u32[]{:S(2)}) copy-start(s32[6]{0:T(128)} %constant.148.clone) | copy-start | bytes 76
  28.2 23.4 %collective-permute-start = (f32[256,256]{1,0:T(8,128)}, f32[256,256]{1,0:T(8,128)S(1)}, u32[]{:S(2)}, u32[]{:S(2)}) collective-permute-start(f32[256,256]{1,0:T(8,128)} %slice_bitcast_fusion.7), channel_id=1, source_target_pairs={{0,4},{4,8},{8,12},{12,16},{16,20},{20,24},{24,28},{28,32},{32,36}... | collective-permute-start | bytes 786440 | tf_op jit(solution)/shard_map/ppermute | solution.py:21
  32.3 20.3 %collective-permute-start.1 = (f32[2,256,128]{2,1,0:T(8,128)}, f32[2,256,128]{2,1,0:T(8,128)S(1)}, u32[]{:S(2)}, u32[]{:S(2)}) collective-permute-start(f32[2,256,128]{2,1,0:T(8,128)} %slice.225), channel_id=1, source_target_pairs={{0,1},{1,2},{2,3},{4,5},{5,6},{6,7},{8,9},{9,10},{10,11},{12,13},{... | collective-permute-start | bytes 786440 | tf_op jit(solution)/shard_map/ppermute | solution.py:21
  42.6 10.1 %copy-start.3 = (f32[2,256,256]{2,1,0:T(8,128)S(1)}, f32[2,256,256]{2,1,0:T(8,128)}, u32[]{:S(2)}) copy-start(f32[2,256,256]{2,1,0:T(8,128)} %slice.224) | copy-start | bytes 1572868
  42.6 10.1 %copy-start.4 = (f32[2,256,128]{2,1,0:T(8,128)S(1)}, f32[2,256,128]{2,1,0:T(8,128)}, u32[]{:S(2)}) copy-start(f32[2,256,128]{2,1,0:T(8,128)} %slice.226) | copy-start | bytes 786436
  54.0 1.3 copy-start
  62.6 11.4 %collective-permute-start.2 = (f32[256,256]{1,0:T(8,128)S(1)}, f32[256,256]{1,0:T(8,128)S(1)}, u32[]{:S(2)}, u32[]{:S(2)}) collective-permute-start(f32[256,256]{1,0:T(8,128)S(1)} %get-tuple-element.48), channel_id=1, source_target_pairs={{4,0},{8,4},{12,8},{16,12},{20,16},{24,20},{28,24},{32,28},{36,32}... | collective-permute-start | bytes 786440 | tf_op jit(solution)/shard_map/ppermute | solution.py:21
  67.1 9.2 %collective-permute-start.5 = (f32[2,256,128]{2,1,0:T(8,128)S(1)}, f32[2,256,128]{2,1,0:T(8,128)S(1)}, u32[]{:S(2)}, u32[]{:S(2)}) collective-permute-start(f32[2,256,128]{2,1,0:T(8,128)S(1)} %get-tuple-element.51), channel_id=1, source_target_pairs={{0,1},{1,2},{2,3},{4,5},{5,6},{6,7},{8,9},{9,10},{10,11},{12,13},{... | collective-permute-start | bytes 786440 | tf_op jit(solution)/shard_map/ppermute | solution.py:21
  70.6 9.8 %collective-permute-start.3 = (f32[2,256,128]{2,1,0:T(8,128)S(1)}, f32[2,256,128]{2,1,0:T(8,128)S(1)}, u32[]{:S(2)}, u32[]{:S(2)}) collective-permute-start(f32[2,256,128]{2,1,0:T(8,128)S(1)} %get-tuple-element.52), channel_id=1, source_target_pairs={{1,0},{2,1},{3,2},{5,4},{6,5},{7,6},{9,8},{10,9},{11,10},{13,12},{... | collective-permute-start | bytes 786440 | tf_op jit(solution)/shard_map/ppermute | solution.py:21
  71.9 8.9 %collective-permute-start.4 = (f32[256,256]{1,0:T(8,128)S(1)}, f32[256,256]{1,0:T(8,128)S(1)}, u32[]{:S(2)}, u32[]{:S(2)}) collective-permute-start(f32[256,256]{1,0:T(8,128)S(1)} %get-tuple-element.47), channel_id=1, source_target_pairs={{0,4},{4,8},{8,12},{12,16},{16,20},{20,24},{24,28},{28,32},{32,36}... | collective-permute-start | bytes 786440 | tf_op jit(solution)/shard_map/ppermute | solution.py:21
  80.9 1.7 %copy-start.2 = (bf16[2,768,768]{2,1,0:T(8,128)(2,1)S(1)}, bf16[2,768,768]{2,1,0:T(8,128)(2,1)}, u32[]{:S(2)}) copy-start(bf16[2,768,768]{2,1,0:T(8,128)(2,1)} %shard_map.69) | copy-start | bytes 7077892
  84.2 10.7 %collective-permute-start.6 = (f32[256,256]{1,0:T(8,128)S(1)}, f32[256,256]{1,0:T(8,128)S(1)}, u32[]{:S(2)}, u32[]{:S(2)}) collective-permute-start(f32[256,256]{1,0:T(8,128)S(1)} %get-tuple-element.40), channel_id=1, source_target_pairs={{4,0},{8,4},{12,8},{16,12},{20,16},{24,20},{28,24},{32,28},{36,32}... | collective-permute-start | bytes 786440 | tf_op jit(solution)/shard_map/ppermute | solution.py:21
  87.4 9.3 %collective-permute-start.9 = (f32[2,256,128]{2,1,0:T(8,128)S(1)}, f32[2,256,128]{2,1,0:T(8,128)S(1)}, u32[]{:S(2)}, u32[]{:S(2)}) collective-permute-start(f32[2,256,128]{2,1,0:T(8,128)S(1)} %get-tuple-element.43), channel_id=1, source_target_pairs={{0,1},{1,2},{2,3},{4,5},{5,6},{6,7},{8,9},{9,10},{10,11},{12,13},{... | collective-permute-start | bytes 786440 | tf_op jit(solution)/shard_map/ppermute | solution.py:21
  91.7 9.2 %collective-permute-start.7 = (f32[2,256,128]{2,1,0:T(8,128)S(1)}, f32[2,256,128]{2,1,0:T(8,128)S(1)}, u32[]{:S(2)}, u32[]{:S(2)}) collective-permute-start(f32[2,256,128]{2,1,0:T(8,128)S(1)} %get-tuple-element.44), channel_id=1, source_target_pairs={{1,0},{2,1},{3,2},{5,4},{6,5},{7,6},{9,8},{10,9},{11,10},{13,12},{... | collective-permute-start | bytes 786440 | tf_op jit(solution)/shard_map/ppermute | solution.py:21
  93.0 8.4 %collective-permute-start.8 = (f32[256,256]{1,0:T(8,128)S(1)}, f32[256,256]{1,0:T(8,128)S(1)}, u32[]{:S(2)}, u32[]{:S(2)}) collective-permute-start(f32[256,256]{1,0:T(8,128)S(1)} %get-tuple-element.39), channel_id=1, source_target_pairs={{0,4},{4,8},{8,12},{12,16},{16,20},{20,24},{24,28},{28,32},{32,36}... | collective-permute-start | bytes 786440 | tf_op jit(solution)/shard_map/ppermute | solution.py:21
  103.5 12.0 %collective-permute-start.10 = (f32[256,256]{1,0:T(8,128)S(1)}, f32[256,256]{1,0:T(8,128)S(1)}, u32[]{:S(2)}, u32[]{:S(2)}) collective-permute-start(f32[256,256]{1,0:T(8,128)S(1)} %get-tuple-element.31), channel_id=1, source_target_pairs={{4,0},{8,4},{12,8},{16,12},{20,16},{24,20},{28,24},{32,28},{36,32}... | collective-permute-start | bytes 786440 | tf_op jit(solution)/shard_map/ppermute | solution.py:21
  107.7 9.9 %collective-permute-start.13 = (f32[2,256,128]{2,1,0:T(8,128)S(1)}, f32[2,256,128]{2,1,0:T(8,128)S(1)}, u32[]{:S(2)}, u32[]{:S(2)}) collective-permute-start(f32[2,256,128]{2,1,0:T(8,128)S(1)} %get-tuple-element.35), channel_id=1, source_target_pairs={{0,1},{1,2},{2,3},{4,5},{5,6},{6,7},{8,9},{9,10},{10,11},{12,13},{... | collective-permute-start | bytes 786440 | tf_op jit(solution)/shard_map/ppermute | solution.py:21
  112.0 9.5 %collective-permute-start.11 = (f32[2,256,128]{2,1,0:T(8,128)S(1)}, f32[2,256,128]{2,1,0:T(8,128)S(1)}, u32[]{:S(2)}, u32[]{:S(2)}) collective-permute-start(f32[2,256,128]{2,1,0:T(8,128)S(1)} %get-tuple-element.36), channel_id=1, source_target_pairs={{1,0},{2,1},{3,2},{5,4},{6,5},{7,6},{9,8},{10,9},{11,10},{13,12},{... | collective-permute-start | bytes 786440 | tf_op jit(solution)/shard_map/ppermute | solution.py:21
  113.4 8.7 %collective-permute-start.12 = (f32[256,256]{1,0:T(8,128)S(1)}, f32[256,256]{1,0:T(8,128)S(1)}, u32[]{:S(2)}, u32[]{:S(2)}) collective-permute-start(f32[256,256]{1,0:T(8,128)S(1)} %get-tuple-element.30), channel_id=1, source_target_pairs={{0,4},{4,8},{8,12},{12,16},{16,20},{20,24},{24,28},{28,32},{32,36}... | collective-permute-start | bytes 786440 | tf_op jit(solution)/shard_map/ppermute | solution.py:21
  124.0 7.7 %collective-permute-start.14 = (f32[256,256]{1,0:T(8,128)S(1)}, f32[256,256]{1,0:T(8,128)S(1)}, u32[]{:S(2)}, u32[]{:S(2)}) collective-permute-start(f32[256,256]{1,0:T(8,128)S(1)} %get-tuple-element.27), channel_id=1, source_target_pairs={{4,0},{8,4},{12,8},{16,12},{20,16},{24,20},{28,24},{32,28},{36,32}... | collective-permute-start | bytes 786440 | tf_op jit(solution)/shard_map/ppermute | solution.py:21
  127.5 10.9 %collective-permute-start.15 = (f32[2,256,128]{2,1,0:T(8,128)S(1)}, f32[2,256,128]{2,1,0:T(8,128)S(1)}, u32[]{:S(2)}, u32[]{:S(2)}) collective-permute-start(f32[2,256,128]{2,1,0:T(8,128)S(1)} %slice.266), channel_id=1, source_target_pairs={{1,0},{2,1},{3,2},{5,4},{6,5},{7,6},{9,8},{10,9},{11,10},{13,12},{... | collective-permute-start | bytes 786440 | tf_op jit(solution)/shard_map/ppermute | solution.py:21
  128.9 9.6 %copy-start.1 = (f32[2,1,256,384]{3,2,1,0:T(8,128)S(1)}, f32[2,1,256,384]{3,2,1,0:T(8,128)}, u32[]{:S(2)}) copy-start(f32[2,1,256,384]{3,2,1,0:T(8,128)} %param.8) | copy-start | bytes 2359300
where the time goes:
time: 141 us; the launch traced here: 140 us
  starting transfers between devices  53.1 us (38%)
  waiting for transfers between devices  35.9 us (25%)
  matrix products  17.2 us (12%)
  other arithmetic  14.8 us (10%)
  local copies, waits for them, and re-layouts  11.4 us (8%)
  Pallas kernels  6.48 us (5%)
    ppermute x16, starting transfers between devices, from_behind(): lax.ppermute(value, axis, [(source, source + steps) for source in range(i...  45.3 us
    ppermute x16, waiting for transfers between devices, from_behind(): lax.ppermute(value, axis, [(source, source + steps) for source in range(i...  35.9 us
    dot_general x1, matrix products, shards(): jnp.einsum('jka,jkb->jab', factor_panels[:, 0, 0], factor_panels[:, 0, 1]...  9.49 us
    all_to_all x1, starting transfers between devices, shards(): lax.all_to_all(send_tiles, 'gx', split_axis=0, concat_axis=0, tiled=True)  7.84 us
    dot_general x4, matrix products, shards(): jnp.einsum('ncm,nmk->nck', jnp.concatenate([high, low], axis=1), matrices...  7.7 us
    pallas_call x1, Pallas kernels, matrix_tiles(): pl.pallas_call(partial(_matrix_kernel, subs=subs, blocks=blocks, block_le...  3.45 us
    pallas_call x1, Pallas kernels, pack_tiles(): pl.pallas_call(partial(_pack_kernel, rows=rows, block_len=block_len), out...  3.03 us
  transfers between devices with their start and end apart: 17, of which 9 were waited for; matrix products, arithmetic and copies ran while one was open for 11% of the time, Pallas kernels for 0%

commit v1 on v0

--- a/solution.py
+++ b/solution.py
@@ -201,11 +201,11 @@
         south_part = image[..., 4 * block_len : 5 * block_len]
         split_north_part = image[..., 5 * block_len :]
         from_east = from_behind(west_part[0], "gx", -1)
-        from_north = from_behind(south_part, "gy", -1)
+        from_north = from_behind(south_part.astype(jnp.bfloat16), "gy", -1).astype(jnp.float32)
         last = sweep == ITERS - 1
         if not last:
             west_east_part = from_behind(split_east_part[sub_count - 1], "gx", 1)
-            south_north_part = from_behind(split_north_part, "gy", 1)
+            south_north_part = from_behind(split_north_part.astype(jnp.bfloat16), "gy", 1).astype(jnp.float32)
         east_near = jnp.concatenate([west_part[1:], from_east[None]], axis=0)
         residual = residual - jnp.concatenate(
             [split_east_part - east_near, split_north_part - from_north], axis=-1

time: 141 us -> 142 us (level)
  the two profiles are of different devices: /device:TPU:17 before, /device:TPU:103 now
where the time goes in v1:
time: 142 us; the launch traced here: 141 us
  starting transfers between devices  50.3 us (35%)
  waiting for transfers between devices  40.1 us (28%)
  matrix products  17.2 us (12%)
  other arithmetic  14.6 us (10%)
  local copies, waits for them, and re-layouts  11.4 us (8%)
  Pallas kernels  6.48 us (5%)
    ppermute x16, starting transfers between devices, from_behind(): lax.ppermute(value, axis, [(source, source + steps) for source in range(i...  42.3 us
    ppermute x16, waiting for transfers between devices, from_behind(): lax.ppermute(value, axis, [(source, source + steps) for source in range(i...  40.1 us
    dot_general x1, matrix products, shards(): jnp.einsum('jka,jkb->jab', factor_panels[:, 0, 0], factor_panels[:, 0, 1]...  9.49 us
    all_to_all x1, starting transfers between devices, shards(): lax.all_to_all(send_tiles, 'gx', split_axis=0, concat_axis=0, tiled=True)  7.98 us
    dot_general x4, matrix products, shards(): jnp.einsum('ncm,nmk->nck', jnp.concatenate([high, low], axis=1), matrices...  7.7 us
    pallas_call x1, Pallas kernels, matrix_tiles(): pl.pallas_call(partial(_matrix_kernel, subs=subs, blocks=blocks, block_le...  3.45 us
    pallas_call x1, Pallas kernels, pack_tiles(): pl.pallas_call(partial(_pack_kernel, rows=rows, block_len=block_len), out...  3.03 us
  transfers between devices with their start and end apart: 17, of which 5 were waited for; matrix products, arithmetic and copies ran while one was open for 11% of the time, Pallas kernels for 0%

profile of v1, /device:TPU:103, one launch (start us, length us, event | category | flops | bytes accessed | tf_op | source)
XLA Modules:
  0.0 141.4 jit_solution(5884709626550074046)
XLA Ops:
  3.7 9.5 %fusion.25.tiles_ref = bf16[26,128,128]{2,1,0:T(8,128)(2,1)} fusion(bf16[26,1,2,1536,128]{4,3,2,1,0:T(8,128)(2,1)} %param.7), kind=kOutput, calls=%fused_computation.41 | convolution fusion | flops 1309048832 | bytes 21299200 | tf_op jit(solution)/shard_map/jka,jkb->jab/dot_general | solution.py:129
  13.8 3.0 %shard_map.68 = bf16[8192,128]{1,0:T(8,128)(2,1)} custom-call(s32[2,64]{1,0:T(2,128)} %pad_add_fusion.1.table_ref, bf16[26,128,128]{2,1,0:T(8,128)(2,1)} %fusion.25.tiles_ref), custom_call_target="tpu_custom_call" | custom-call | bytes 2949120 | tf_op jit(solution)/shard_map/pallas_call | solution.py:34
  16.8 8.0 %all-to-all-start = ((bf16[32,256,128]{2,1,0:T(8,128)(2,1)}), bf16[32,256,128]{2,1,0:T(8,128)(2,1)S(1)}, u32[]{:S(2)}, u32[]{:S(2)}) async-start(bf16[32,256,128]{2,1,0:T(8,128)(2,1)} %bitcast.137), calls=%async_computation | async-start | bytes 4194304 | tf_op jit(solution)/shard_map/all_to_all | solution.py:154
  25.5 2.1 %broadcast_multiply_fusion = (f32[2,256,384]{2,1,0:T(8,128)}, f32[2,256,384]{2,1,0:T(8,128)S(1)}) fusion(f32[2,384]{1,0:T(2,128)S(1)} %pad_convert_fusion, f32[2,1,256,384]{3,2,1,0:T(8,128)} %param.8), kind=kLoop, calls=%fused_computation.66 | loop fusion | flops 393216 | bytes 2362368 | tf_op jit(solution)/shard_map/div | solution.py:179
  28.3 3.4 %collective-permute-start = (f32[256,256]{1,0:T(8,128)}, f32[256,256]{1,0:T(8,128)S(1)}, u32[]{:S(2)}, u32[]{:S(2)}) collective-permute-start(f32[256,256]{1,0:T(8,128)} %slice_bitcast_fusion.7), channel_id=1, source_target_pairs={{0,4},{4,8},{8,12},{12,16},{16,20},{20,24},{24,28},{28,32},{32,36}... | collective-permute-start | bytes 786440 | tf_op jit(solution)/shard_map/ppermute | solution.py:21
  33.8 1.7 %slice.227 = f32[2,256,128]{2,1,0:T(8,128)} slice(f32[2,256,384]{2,1,0:T(8,128)} %get-tuple-element.16), slice={[0:2], [0:256], [256:384]} | slice | bytes 524288 | tf_op jit(solution)/shard_map/slice | solution.py:186
  35.5 1.7 %slice.224 = f32[1,256,256]{2,1,0:T(8,128)} slice(f32[2,256,384]{2,1,0:T(8,128)} %get-tuple-element.16), slice={[0:1], [0:256], [0:256]} | slice | bytes 524288 | tf_op jit(solution)/shard_map/slice | solution.py:187
  37.2 1.9 %slice.225 = f32[2,256,256]{2,1,0:T(8,128)} slice(f32[2,256,384]{2,1,0:T(8,128)} %get-tuple-element.16), slice={[0:2], [0:256], [0:256]} | slice | bytes 1048576 | tf_op jit(solution)/shard_map/slice | solution.py:185
  41.1 9.7 %collective-permute-done = f32[256,256]{1,0:T(8,128)S(1)} collective-permute-done((f32[256,256]{1,0:T(8,128)}, f32[256,256]{1,0:T(8,128)S(1)}, u32[]{:S(2)}, u32[]{:S(2)}) %collective-permute-start) | collective-permute-done | bytes 262176 | tf_op jit(solution)/shard_map/ppermute | solution.py:21
  51.8 1.4 reduce-precision_convert_fusion.3
  54.6 3.5 %shard_map.69 = bf16[2,768,768]{2,1,0:T(8,128)(2,1)} custom-call(s32[2,72]{1,0:T(2,128)} %pad_add_fusion.table_ref, bf16[64,128,128]{2,1,0:T(8,128)(2,1)} %bitcast.136), custom_call_target="tpu_custom_call" | custom-call | bytes 4456448 | tf_op jit(solution)/shard_map/pallas_call | solution.py:67
  58.0 3.5 %fusion.9 = f32[2,512,768]{2,1,0:T(8,128)S(1)} fusion(bf16[2,768,768]{2,1,0:T(8,128)(2,1)} %shard_map.69, bf16[2,256,768]{2,1,0:T(8,128)(2,1)} %get-tuple-element.54, bf16[2,256,768]{2,1,0:T(8,128)(2,1)} %get-tuple-element.53), kind=kOutput, calls=%fused_computation.22 | convolution fusion | flops 1211105280 | bytes 7077888 | tf_op jit(solution)/shard_map/ncm,nmk->nck/dot_general | solution.py:192
  63.1 4.0 %collective-permute-start.3 = (bf16[2,256,128]{2,1,0:T(8,128)(2,1)S(1)}, bf16[2,256,128]{2,1,0:T(8,128)(2,1)S(1)}, u32[]{:S(2)}, u32[]{:S(2)}) collective-permute-start(bf16[2,256,128]{2,1,0:T(8,128)(2,1)S(1)} %get-tuple-element.52), channel_id=1, source_target_pairs={{1,0},{2,1},{3,2},{5,4},{6,5},{7,6},{9,8},{10,9},{11,10},{13,12},{... | collective-permute-start | bytes 393224 | tf_op jit(solution)/shard_map/ppermute | solution.py:21
  67.2 7.0 %collective-permute-start.4 = (f32[256,256]{1,0:T(8,128)S(1)}, f32[256,256]{1,0:T(8,128)S(1)}, u32[]{:S(2)}, u32[]{:S(2)}) collective-permute-start(f32[256,256]{1,0:T(8,128)S(1)} %get-tuple-element.47), channel_id=1, source_target_pairs={{0,4},{4,8},{8,12},{12,16},{16,20},{20,24},{24,28},{28,32},{32,36}... | collective-permute-start | bytes 786440 | tf_op jit(solution)/shard_map/ppermute | solution.py:21
  74.1 1.9 %collective-permute-start.2 = (f32[256,256]{1,0:T(8,128)S(1)}, f32[256,256]{1,0:T(8,128)S(1)}, u32[]{:S(2)}, u32[]{:S(2)}) collective-permute-start(f32[256,256]{1,0:T(8,128)S(1)} %get-tuple-element.48), channel_id=1, source_target_pairs={{4,0},{8,4},{12,8},{16,12},{20,16},{24,20},{28,24},{32,28},{36,32}... | collective-permute-start | bytes 786440 | tf_op jit(solution)/shard_map/ppermute | solution.py:21
  76.2 7.7 %collective-permute-done.2 = f32[256,256]{1,0:T(8,128)S(1)} collective-permute-done((f32[256,256]{1,0:T(8,128)S(1)}, f32[256,256]{1,0:T(8,128)S(1)}, u32[]{:S(2)}, u32[]{:S(2)}) %collective-permute-start.2) | collective-permute-done | bytes 262176 | tf_op jit(solution)/shard_map/ppermute | solution.py:21
  84.6 1.4 %copy-done.2 = bf16[2,768,768]{2,1,0:T(8,128)(2,1)S(1)} copy-done((bf16[2,768,768]{2,1,0:T(8,128)(2,1)S(1)}, bf16[2,768,768]{2,1,0:T(8,128)(2,1)}, u32[]{:S(2)}) %copy-start.2) | copy-done | bytes 2359320
  86.0 1.4 fusion.13
  89.0 4.0 %collective-permute-start.7 = (bf16[2,256,128]{2,1,0:T(8,128)(2,1)S(1)}, bf16[2,256,128]{2,1,0:T(8,128)(2,1)S(1)}, u32[]{:S(2)}, u32[]{:S(2)}) collective-permute-start(bf16[2,256,128]{2,1,0:T(8,128)(2,1)S(1)} %get-tuple-element.44), channel_id=1, source_target_pairs={{1,0},{2,1},{3,2},{5,4},{6,5},{7,6},{9,8},{10,9},{11,10},{13,12},{... | collective-permute-start | bytes 393224 | tf_op jit(solution)/shard_map/ppermute | solution.py:21
  93.0 2.3 %collective-permute-start.8 = (f32[256,256]{1,0:T(8,128)S(1)}, f32[256,256]{1,0:T(8,128)S(1)}, u32[]{:S(2)}, u32[]{:S(2)}) collective-permute-start(f32[256,256]{1,0:T(8,128)S(1)} %get-tuple-element.39), channel_id=1, source_target_pairs={{0,4},{4,8},{8,12},{12,16},{16,20},{20,24},{24,28},{28,32},{32,36}... | collective-permute-start | bytes 786440 | tf_op jit(solution)/shard_map/ppermute | solution.py:21
  95.3 2.0 %collective-permute-start.6 = (f32[256,256]{1,0:T(8,128)S(1)}, f32[256,256]{1,0:T(8,128)S(1)}, u32[]{:S(2)}, u32[]{:S(2)}) collective-permute-start(f32[256,256]{1,0:T(8,128)S(1)} %get-tuple-element.40), channel_id=1, source_target_pairs={{4,0},{8,4},{12,8},{16,12},{20,16},{24,20},{28,24},{32,28},{36,32}... | collective-permute-start | bytes 786440 | tf_op jit(solution)/shard_map/ppermute | solution.py:21
  97.6 7.5 %collective-permute-done.6 = f32[256,256]{1,0:T(8,128)S(1)} collective-permute-done((f32[256,256]{1,0:T(8,128)S(1)}, f32[256,256]{1,0:T(8,128)S(1)}, u32[]{:S(2)}, u32[]{:S(2)}) %collective-permute-start.6) | collective-permute-done | bytes 262176 | tf_op jit(solution)/shard_map/ppermute | solution.py:21
  106.0 1.4 fusion.17
  109.0 4.0 %collective-permute-start.11 = (bf16[2,256,128]{2,1,0:T(8,128)(2,1)S(1)}, bf16[2,256,128]{2,1,0:T(8,128)(2,1)S(1)}, u32[]{:S(2)}, u32[]{:S(2)}) collective-permute-start(bf16[2,256,128]{2,1,0:T(8,128)(2,1)S(1)} %get-tuple-element.36), channel_id=1, source_target_pairs={{1,0},{2,1},{3,2},{5,4},{6,5},{7,6},{9,8},{10,9},{11,10},{13,12},{... | collective-permute-start | bytes 393224 | tf_op jit(solution)/shard_map/ppermute | solution.py:21
  113.0 2.3 %collective-permute-start.12 = (f32[256,256]{1,0:T(8,128)S(1)}, f32[256,256]{1,0:T(8,128)S(1)}, u32[]{:S(2)}, u32[]{:S(2)}) collective-permute-start(f32[256,256]{1,0:T(8,128)S(1)} %get-tuple-element.30), channel_id=1, source_target_pairs={{0,4},{4,8},{8,12},{12,16},{16,20},{20,24},{24,28},{28,32},{32,36}... | collective-permute-start | bytes 786440 | tf_op jit(solution)/shard_map/ppermute | solution.py:21
  115.3 2.2 %collective-permute-start.10 = (f32[256,256]{1,0:T(8,128)S(1)}, f32[256,256]{1,0:T(8,128)S(1)}, u32[]{:S(2)}, u32[]{:S(2)}) collective-permute-start(f32[256,256]{1,0:T(8,128)S(1)} %get-tuple-element.31), channel_id=1, source_target_pairs={{4,0},{8,4},{12,8},{16,12},{20,16},{24,20},{28,24},{32,28},{36,32}... | collective-permute-start | bytes 786440 | tf_op jit(solution)/shard_map/ppermute | solution.py:21
  117.8 7.3 %collective-permute-done.10 = f32[256,256]{1,0:T(8,128)S(1)} collective-permute-done((f32[256,256]{1,0:T(8,128)S(1)}, f32[256,256]{1,0:T(8,128)S(1)}, u32[]{:S(2)}, u32[]{:S(2)}) %collective-permute-start.10) | collective-permute-done | bytes 262176 | tf_op jit(solution)/shard_map/ppermute | solution.py:21
  126.0 1.4 fusion.21
  127.7 2.0 %collective-permute-start.15 = (bf16[2,256,128]{2,1,0:T(8,128)(2,1)S(1)}, bf16[2,256,128]{2,1,0:T(8,128)(2,1)S(1)}, u32[]{:S(2)}, u32[]{:S(2)}) collective-permute-start(bf16[2,256,128]{2,1,0:T(8,128)(2,1)S(1)} %slice.333), channel_id=1, source_target_pairs={{1,0},{2,1},{3,2},{5,4},{6,5},{7,6},{9,8},{10,9},{11,10},{13,12},{... | collective-permute-start | bytes 393224 | tf_op jit(solution)/shard_map/ppermute | solution.py:21
  129.7 2.1 %collective-permute-start.14 = (f32[256,256]{1,0:T(8,128)S(1)}, f32[256,256]{1,0:T(8,128)S(1)}, u32[]{:S(2)}, u32[]{:S(2)}) collective-permute-start(f32[256,256]{1,0:T(8,128)S(1)} %get-tuple-element.27), channel_id=1, source_target_pairs={{4,0},{8,4},{12,8},{16,12},{20,16},{24,20},{28,24},{32,28},{36,32}... | collective-permute-start | bytes 786440 | tf_op jit(solution)/shard_map/ppermute | solution.py:21
  131.9 7.8 %collective-permute-done.14 = f32[256,256]{1,0:T(8,128)S(1)} collective-permute-done((f32[256,256]{1,0:T(8,128)S(1)}, f32[256,256]{1,0:T(8,128)S(1)}, u32[]{:S(2)}, u32[]{:S(2)}) %collective-permute-start.14) | collective-permute-done | bytes 262176 | tf_op jit(solution)/shard_map/ppermute | solution.py:21
  139.7 1.6 %fusion.32 = (f32[2,1,256,384]{3,2,1,0:T(8,128)}, f32[2,1,256,384]{3,2,1,0:T(8,128)}) fusion(f32[2,1,256,128]{3,2,0,1:T(8,128)S(1)} %fusion.34, f32[2,1,256,256]{3,2,0,1:T(8,128)S(1)} %fusion.33, f32[2,1,256,128]{3,2,0,1:T(8,128)S(1)} %bitcast.141, f32[2,1,256,256]{3,2,0,1:T(8,128)S(1)} %fusion.65, f32[2,1,256,128]{3,2,0,1:T(8,128)S(1)} %bitcast.139, ...), kind=kLoop, calls=%fused_computation.51 | loop fusion | flops 4325376 | bytes 5508096
  (122 shorter events, 19.4 us)
Async XLA Ops:
  16.8 8.0 %copy-start.5 = (s32[64,1]{0,1:T(1,128)S(1)}, s32[64,1]{0,1:T(1,128)}, u32[]{:S(2)}) copy-start(s32[64,1]{0,1:T(1,128)} %param.5) | copy-start | bytes 772
  16.8 36.4 %all-to-all-start = ((bf16[32,256,128]{2,1,0:T(8,128)(2,1)}), bf16[32,256,128]{2,1,0:T(8,128)(2,1)S(1)}, u32[]{:S(2)}, u32[]{:S(2)}) async-start(bf16[32,256,128]{2,1,0:T(8,128)(2,1)} %bitcast.137), calls=%async_computation | async-start | bytes 4194304 | tf_op jit(solution)/shard_map/all_to_all | solution.py:154
  27.6 12.0 %copy-start.6 = (s32[6]{0:T(128)S(1)}, s32[6]{0:T(128)}, u32[]{:S(2)}) copy-start(s32[6]{0:T(128)} %constant.148.clone) | copy-start | bytes 76
  28.3 22.4 %collective-permute-start = (f32[256,256]{1,0:T(8,128)}, f32[256,256]{1,0:T(8,128)S(1)}, u32[]{:S(2)}, u32[]{:S(2)}) collective-permute-start(f32[256,256]{1,0:T(8,128)} %slice_bitcast_fusion.7), channel_id=1, source_target_pairs={{0,4},{4,8},{8,12},{12,16},{16,20},{20,24},{24,28},{28,32},{32,36}... | collective-permute-start | bytes 786440 | tf_op jit(solution)/shard_map/ppermute | solution.py:21
  32.4 19.4 %collective-permute-start.1 = (f32[2,256,128]{2,1,0:T(8,128)}, f32[2,256,128]{2,1,0:T(8,128)S(1)}, u32[]{:S(2)}, u32[]{:S(2)}) collective-permute-start(f32[2,256,128]{2,1,0:T(8,128)} %slice.226), channel_id=1, source_target_pairs={{0,1},{1,2},{2,3},{4,5},{5,6},{6,7},{8,9},{9,10},{10,11},{12,13},{... | collective-permute-start | bytes 786440 | tf_op jit(solution)/shard_map/ppermute | solution.py:21
  40.4 11.4 %copy-start.3 = (f32[2,256,256]{2,1,0:T(8,128)S(1)}, f32[2,256,256]{2,1,0:T(8,128)}, u32[]{:S(2)}) copy-start(f32[2,256,256]{2,1,0:T(8,128)} %slice.225) | copy-start | bytes 1572868
  40.4 11.4 %copy-start.4 = (f32[2,256,128]{2,1,0:T(8,128)S(1)}, f32[2,256,128]{2,1,0:T(8,128)}, u32[]{:S(2)}) copy-start(f32[2,256,128]{2,1,0:T(8,128)} %slice.227) | copy-start | bytes 786436
  53.2 1.3 copy-start
  61.8 14.3 %collective-permute-start.5 = (bf16[2,256,128]{2,1,0:T(8,128)(2,1)S(1)}, bf16[2,256,128]{2,1,0:T(8,128)(2,1)S(1)}, u32[]{:S(2)}, u32[]{:S(2)}) collective-permute-start(bf16[2,256,128]{2,1,0:T(8,128)(2,1)S(1)} %get-tuple-element.51), channel_id=1, source_target_pairs={{0,1},{1,2},{2,3},{4,5},{5,6},{6,7},{8,9},{9,10},{10,11},{12,13},{... | collective-permute-start | bytes 393224 | tf_op jit(solution)/shard_map/ppermute | solution.py:21
  63.1 13.0 %collective-permute-start.3 = (bf16[2,256,128]{2,1,0:T(8,128)(2,1)S(1)}, bf16[2,256,128]{2,1,0:T(8,128)(2,1)S(1)}, u32[]{:S(2)}, u32[]{:S(2)}) collective-permute-start(bf16[2,256,128]{2,1,0:T(8,128)(2,1)S(1)} %get-tuple-element.52), channel_id=1, source_target_pairs={{1,0},{2,1},{3,2},{5,4},{6,5},{7,6},{9,8},{10,9},{11,10},{13,12},{... | collective-permute-start | bytes 393224 | tf_op jit(solution)/shard_map/ppermute | solution.py:21
  67.2 17.1 %collective-permute-start.4 = (f32[256,256]{1,0:T(8,128)S(1)}, f32[256,256]{1,0:T(8,128)S(1)}, u32[]{:S(2)}, u32[]{:S(2)}) collective-permute-start(f32[256,256]{1,0:T(8,128)S(1)} %get-tuple-element.47), channel_id=1, source_target_pairs={{0,4},{4,8},{8,12},{12,16},{16,20},{20,24},{24,28},{28,32},{32,36}... | collective-permute-start | bytes 786440 | tf_op jit(solution)/shard_map/ppermute | solution.py:21
  74.1 9.8 %collective-permute-start.2 = (f32[256,256]{1,0:T(8,128)S(1)}, f32[256,256]{1,0:T(8,128)S(1)}, u32[]{:S(2)}, u32[]{:S(2)}) collective-permute-start(f32[256,256]{1,0:T(8,128)S(1)} %get-tuple-element.48), channel_id=1, source_target_pairs={{4,0},{8,4},{12,8},{16,12},{20,16},{24,20},{28,24},{32,28},{36,32}... | collective-permute-start | bytes 786440 | tf_op jit(solution)/shard_map/ppermute | solution.py:21
  84.4 1.7 %copy-start.2 = (bf16[2,768,768]{2,1,0:T(8,128)(2,1)S(1)}, bf16[2,768,768]{2,1,0:T(8,128)(2,1)}, u32[]{:S(2)}) copy-start(bf16[2,768,768]{2,1,0:T(8,128)(2,1)} %shard_map.69) | copy-start | bytes 7077892
  87.7 9.7 %collective-permute-start.9 = (bf16[2,256,128]{2,1,0:T(8,128)(2,1)S(1)}, bf16[2,256,128]{2,1,0:T(8,128)(2,1)S(1)}, u32[]{:S(2)}, u32[]{:S(2)}) collective-permute-start(bf16[2,256,128]{2,1,0:T(8,128)(2,1)S(1)} %get-tuple-element.43), channel_id=1, source_target_pairs={{0,1},{1,2},{2,3},{4,5},{5,6},{6,7},{8,9},{9,10},{10,11},{12,13},{... | collective-permute-start | bytes 393224 | tf_op jit(solution)/shard_map/ppermute | solution.py:21
  89.0 8.4 %collective-permute-start.7 = (bf16[2,256,128]{2,1,0:T(8,128)(2,1)S(1)}, bf16[2,256,128]{2,1,0:T(8,128)(2,1)S(1)}, u32[]{:S(2)}, u32[]{:S(2)}) collective-permute-start(bf16[2,256,128]{2,1,0:T(8,128)(2,1)S(1)} %get-tuple-element.44), channel_id=1, source_target_pairs={{1,0},{2,1},{3,2},{5,4},{6,5},{7,6},{9,8},{10,9},{11,10},{13,12},{... | collective-permute-start | bytes 393224 | tf_op jit(solution)/shard_map/ppermute | solution.py:21
  93.0 12.6 %collective-permute-start.8 = (f32[256,256]{1,0:T(8,128)S(1)}, f32[256,256]{1,0:T(8,128)S(1)}, u32[]{:S(2)}, u32[]{:S(2)}) collective-permute-start(f32[256,256]{1,0:T(8,128)S(1)} %get-tuple-element.39), channel_id=1, source_target_pairs={{0,4},{4,8},{8,12},{12,16},{16,20},{20,24},{24,28},{28,32},{32,36}... | collective-permute-start | bytes 786440 | tf_op jit(solution)/shard_map/ppermute | solution.py:21
  95.3 9.8 %collective-permute-start.6 = (f32[256,256]{1,0:T(8,128)S(1)}, f32[256,256]{1,0:T(8,128)S(1)}, u32[]{:S(2)}, u32[]{:S(2)}) collective-permute-start(f32[256,256]{1,0:T(8,128)S(1)} %get-tuple-element.40), channel_id=1, source_target_pairs={{4,0},{8,4},{12,8},{16,12},{20,16},{24,20},{28,24},{32,28},{36,32}... | collective-permute-start | bytes 786440 | tf_op jit(solution)/shard_map/ppermute | solution.py:21
  107.7 9.9 %collective-permute-start.13 = (bf16[2,256,128]{2,1,0:T(8,128)(2,1)S(1)}, bf16[2,256,128]{2,1,0:T(8,128)(2,1)S(1)}, u32[]{:S(2)}, u32[]{:S(2)}) collective-permute-start(bf16[2,256,128]{2,1,0:T(8,128)(2,1)S(1)} %get-tuple-element.35), channel_id=1, source_target_pairs={{0,1},{1,2},{2,3},{4,5},{5,6},{6,7},{8,9},{9,10},{10,11},{12,13},{... | collective-permute-start | bytes 393224 | tf_op jit(solution)/shard_map/ppermute | solution.py:21
  109.0 8.6 %collective-permute-start.11 = (bf16[2,256,128]{2,1,0:T(8,128)(2,1)S(1)}, bf16[2,256,128]{2,1,0:T(8,128)(2,1)S(1)}, u32[]{:S(2)}, u32[]{:S(2)}) collective-permute-start(bf16[2,256,128]{2,1,0:T(8,128)(2,1)S(1)} %get-tuple-element.36), channel_id=1, source_target_pairs={{1,0},{2,1},{3,2},{5,4},{6,5},{7,6},{9,8},{10,9},{11,10},{13,12},{... | collective-permute-start | bytes 393224 | tf_op jit(solution)/shard_map/ppermute | solution.py:21
  113.0 12.6 %collective-permute-start.12 = (f32[256,256]{1,0:T(8,128)S(1)}, f32[256,256]{1,0:T(8,128)S(1)}, u32[]{:S(2)}, u32[]{:S(2)}) collective-permute-start(f32[256,256]{1,0:T(8,128)S(1)} %get-tuple-element.30), channel_id=1, source_target_pairs={{0,4},{4,8},{8,12},{12,16},{16,20},{20,24},{24,28},{28,32},{32,36}... | collective-permute-start | bytes 786440 | tf_op jit(solution)/shard_map/ppermute | solution.py:21
  115.3 9.8 %collective-permute-start.10 = (f32[256,256]{1,0:T(8,128)S(1)}, f32[256,256]{1,0:T(8,128)S(1)}, u32[]{:S(2)}, u32[]{:S(2)}) collective-permute-start(f32[256,256]{1,0:T(8,128)S(1)} %get-tuple-element.31), channel_id=1, source_target_pairs={{4,0},{8,4},{12,8},{16,12},{20,16},{24,20},{28,24},{32,28},{36,32}... | collective-permute-start | bytes 786440 | tf_op jit(solution)/shard_map/ppermute | solution.py:21
  127.7 4.2 %collective-permute-start.15 = (bf16[2,256,128]{2,1,0:T(8,128)(2,1)S(1)}, bf16[2,256,128]{2,1,0:T(8,128)(2,1)S(1)}, u32[]{:S(2)}, u32[]{:S(2)}) collective-permute-start(bf16[2,256,128]{2,1,0:T(8,128)(2,1)S(1)} %slice.333), channel_id=1, source_target_pairs={{1,0},{2,1},{3,2},{5,4},{6,5},{7,6},{9,8},{10,9},{11,10},{13,12},{... | collective-permute-start | bytes 393224 | tf_op jit(solution)/shard_map/ppermute | solution.py:21
  129.7 10.0 %copy-start.1 = (f32[2,1,256,384]{3,2,1,0:T(8,128)S(1)}, f32[2,1,256,384]{3,2,1,0:T(8,128)}, u32[]{:S(2)}) copy-start(f32[2,1,256,384]{3,2,1,0:T(8,128)} %param.8) | copy-start | bytes 2359300
  129.7 9.9 %collective-permute-start.14 = (f32[256,256]{1,0:T(8,128)S(1)}, f32[256,256]{1,0:T(8,128)S(1)}, u32[]{:S(2)}, u32[]{:S(2)}) collective-permute-start(f32[256,256]{1,0:T(8,128)S(1)} %get-tuple-element.27), channel_id=1, source_target_pairs={{4,0},{8,4},{12,8},{16,12},{20,16},{24,20},{28,24},{32,28},{36,32}... | collective-permute-start | bytes 786440 | tf_op jit(solution)/shard_map/ppermute | solution.py:21

commit v2 on v0

--- a/solution.py
+++ b/solution.py
@@ -21,18 +21,28 @@
     return lax.ppermute(value, axis, [(source, source + steps) for source in range(initial, last)])
 
 
-def _pack_kernel(table_ref, tiles_ref, out_ref, *, rows, block_len):
-    for r in range(rows):
-        tile = tiles_ref[table_ref[0, r]]
-        keep = table_ref[1, r] != 0
-        out_ref[r * block_len : (r + 1) * block_len, :] = jnp.where(keep, tile, jnp.zeros_like(tile))
-
-
-def pack_tiles(table, tiles, rows):
+def _pack_kernel(code_ref, tiles_ref, out_ref, *, per_owner, owner_subs, block_len):
+    out_ref[...] = jnp.zeros_like(out_ref)
+    previous = jnp.int32(-1)
+    rank = jnp.int32(0)
+    for j in range(tiles_ref.shape[0]):
+        code = code_ref[j]
+        owner = lax.div(jnp.maximum(code, 0), jnp.int32(NB * NB * owner_subs))
+        rank = jnp.where(owner == previous, rank + 1, 0)
+        previous = owner
+        slot = owner * per_owner + rank
+
+        @pl.when((code >= 0) & (rank < per_owner))
+        def _():
+            out_ref[pl.ds(pl.multiple_of(slot * block_len, block_len), block_len), :] = tiles_ref[j]
+
+
+def pack_tiles(codes, tiles, owners, per_owner, owner_subs):
     block_len = tiles.shape[-1]
+    rows = owners * per_owner
     size = 2 * block_len * block_len
     return pl.pallas_call(
-        partial(_pack_kernel, rows=rows, block_len=block_len),
+        partial(_pack_kernel, per_owner=per_owner, owner_subs=owner_subs, block_len=block_len),
         out_shape=jax.ShapeDtypeStruct((rows * block_len, block_len), tiles.dtype),
         in_specs=[
             pl.BlockSpec(memory_space=pltpu.SMEM),
@@ -42,7 +52,7 @@
         cost_estimate=pl.CostEstimate(
             flops=0, transcendentals=0, bytes_accessed=(tiles.shape[0] + rows) * size
         ),
-    )(table, tiles)
+    )(codes, tiles)
 
 
 def _matrix_kernel(table_ref, tiles_ref, out_ref, *, subs, blocks, block_len):
@@ -132,24 +142,9 @@
         factor_panels[:, 0, 1],
         preferred_element_type=jnp.float32,
     ).astype(jnp.bfloat16)
-    tile_codes = job_code[:, 0]
-    job_count = tile_codes.shape[0]
-    is_valid = tile_codes >= 0
-    owner_gx = jnp.where(is_valid, tile_codes // (NB * NB) // sub_count, 0)
     slot_cap = (sub_count * NB * (NB + 1) // 2 + gx_count - 1) // gx_count
-    job_order = jnp.arange(job_count, dtype=jnp.int32)
-    same_owner = (
-        (owner_gx[:, None] == owner_gx[None, :])
-        & is_valid[None, :]
-        & (job_order[None, :] < job_order[:, None])
-    )
-    slot_rank = jnp.sum(same_owner.astype(jnp.int32), axis=1)
-    send_slot = jnp.where(is_valid & (slot_rank < slot_cap), owner_gx * slot_cap + slot_rank, -1)
     slot_count = gx_count * slot_cap
-    send_hit = send_slot[None, :] == jnp.arange(slot_count, dtype=jnp.int32)[:, None]
-    send_from = jnp.sum(jnp.where(send_hit, job_order[None, :], 0), axis=1)
-    send_mode = jnp.any(send_hit, axis=1).astype(jnp.int32)
-    send_tiles = pack_tiles(jnp.stack([send_from, send_mode]), tiles, slot_count)
+    send_tiles = pack_tiles(job_code[:, 0], tiles, gx_count, slot_cap, sub_count)
     send_tiles = send_tiles.reshape(gx_count, slot_cap * block_len, block_len)
     got_tiles = lax.all_to_all(send_tiles, "gx", split_axis=0, concat_axis=0, tiled=True)
     got_tiles = got_tiles.reshape(slot_count, block_len, block_len)

time: 141 us -> 137 us (0.972)
  other arithmetic: 14.8 us -> 10.9 us
  transfers between devices with their start and end apart: 17 -> 17, of which waited for: 9 -> 9; matrix products, arithmetic and copies ran while one was open for 11% -> 12% of each run, Pallas kernels for 0% -> 0%
where the time goes in v2:
time: 137 us
  starting transfers between devices  53.1 us (39%)
  waiting for transfers between devices  36 us (26%)
  matrix products  17.2 us (13%)
  local copies, waits for them, and re-layouts  11.4 us (8%)
  other arithmetic  10.9 us (8%)
  Pallas kernels  6.6 us (5%)
    ppermute x16, starting transfers between devices, from_behind(): lax.ppermute(value, axis, [(source, source + steps) for source in range(i...  45.3 us
    ppermute x16, waiting for transfers between devices, from_behind(): lax.ppermute(value, axis, [(source, source + steps) for source in range(i...  36 us
    dot_general x1, matrix products, shards(): jnp.einsum('jka,jkb->jab', factor_panels[:, 0, 0], factor_panels[:, 0, 1]...  9.51 us
    all_to_all x1, starting transfers between devices, shards(): lax.all_to_all(send_tiles, 'gx', split_axis=0, concat_axis=0, tiled=True)  7.85 us
    dot_general x4, matrix products, shards(): jnp.einsum('ncm,nmk->nck', jnp.concatenate([high, low], axis=1), matrices...  7.7 us
    pallas_call x1, Pallas kernels, matrix_tiles(): pl.pallas_call(partial(_matrix_kernel, subs=subs, blocks=blocks, block_le...  3.46 us
    pallas_call x1, Pallas kernels, pack_tiles(): pl.pallas_call(partial(_pack_kernel, per_owner=per_owner, owner_subs=owne...  3.14 us
    unnamed x14, local copies, waits for them, and re-layouts  2.8 us
  transfers between devices with their start and end apart: 17, of which 9 were waited for; matrix products, arithmetic and copies ran while one was open for 12% of the time, Pallas kernels for 0%

profile of v2, /device:TPU:17, one launch (start us, length us, event | category | flops | bytes accessed | tf_op | source)
XLA Modules:
  0.0 136.5 jit_solution(1356069558765086689)
XLA Ops:
  0.6 9.5 %fusion.25.tiles_ref = bf16[26,128,128]{2,1,0:T(8,128)(2,1)} fusion(bf16[26,1,2,1536,128]{4,3,2,1,0:T(8,128)(2,1)} %param.7), kind=kOutput, calls=%fused_computation.41 | convolution fusion | flops 1309048832 | bytes 21299200 | tf_op jit(solution)/shard_map/jka,jkb->jab/dot_general | solution.py:139
  10.1 3.1 %shard_map.68 = bf16[8192,128]{1,0:T(8,128)(2,1)} custom-call(s32[26]{0:T(128)} %bitcast.127, bf16[26,128,128]{2,1,0:T(8,128)(2,1)} %fusion.25.tiles_ref), custom_call_target="tpu_custom_call" | custom-call | bytes 2949120 | tf_op jit(solution)/shard_map/pallas_call | solution.py:44
  13.3 7.8 %all-to-all-start = ((bf16[32,256,128]{2,1,0:T(8,128)(2,1)}), bf16[32,256,128]{2,1,0:T(8,128)(2,1)S(1)}, u32[]{:S(2)}, u32[]{:S(2)}) async-start(bf16[32,256,128]{2,1,0:T(8,128)(2,1)} %bitcast.113), calls=%async_computation | async-start | bytes 4194304 | tf_op jit(solution)/shard_map/all_to_all | solution.py:149
  21.8 2.1 %broadcast_multiply_fusion = (f32[2,256,384]{2,1,0:T(8,128)}, f32[2,256,384]{2,1,0:T(8,128)S(1)}) fusion(f32[2,384]{1,0:T(2,128)S(1)} %pad_convert_fusion, f32[2,1,256,384]{3,2,1,0:T(8,128)} %param.8), kind=kLoop, calls=%fused_computation.66 | loop fusion | flops 393216 | bytes 2362368 | tf_op jit(solution)/shard_map/div | solution.py:174
  24.7 3.4 %collective-permute-start = (f32[256,256]{1,0:T(8,128)}, f32[256,256]{1,0:T(8,128)S(1)}, u32[]{:S(2)}, u32[]{:S(2)}) collective-permute-start(f32[256,256]{1,0:T(8,128)} %slice_bitcast_fusion.7), channel_id=1, source_target_pairs={{0,4},{4,8},{8,12},{12,16},{16,20},{20,24},{24,28},{28,32},{32,36}... | collective-permute-start | bytes 786440 | tf_op jit(solution)/shard_map/ppermute | solution.py:21
  28.8 3.5 %collective-permute-start.1 = (f32[2,256,128]{2,1,0:T(8,128)}, f32[2,256,128]{2,1,0:T(8,128)S(1)}, u32[]{:S(2)}, u32[]{:S(2)}) collective-permute-start(f32[2,256,128]{2,1,0:T(8,128)} %slice.225), channel_id=1, source_target_pairs={{0,1},{1,2},{2,3},{4,5},{5,6},{6,7},{8,9},{9,10},{10,11},{12,13},{... | collective-permute-start | bytes 786440 | tf_op jit(solution)/shard_map/ppermute | solution.py:21
  32.4 1.7 %slice.226 = f32[2,256,128]{2,1,0:T(8,128)} slice(f32[2,256,384]{2,1,0:T(8,128)} %get-tuple-element.14), slice={[0:2], [0:256], [256:384]} | slice | bytes 524288 | tf_op jit(solution)/shard_map/slice | solution.py:181
  34.1 1.7 %slice.223 = f32[1,256,256]{2,1,0:T(8,128)} slice(f32[2,256,384]{2,1,0:T(8,128)} %get-tuple-element.14), slice={[0:1], [0:256], [0:256]} | slice | bytes 524288 | tf_op jit(solution)/shard_map/slice | solution.py:182
  35.8 1.9 %slice.224 = f32[2,256,256]{2,1,0:T(8,128)} slice(f32[2,256,384]{2,1,0:T(8,128)} %get-tuple-element.14), slice={[0:2], [0:256], [0:256]} | slice | bytes 1048576 | tf_op jit(solution)/shard_map/slice | solution.py:180
  39.7 8.3 %collective-permute-done = f32[256,256]{1,0:T(8,128)S(1)} collective-permute-done((f32[256,256]{1,0:T(8,128)}, f32[256,256]{1,0:T(8,128)S(1)}, u32[]{:S(2)}, u32[]{:S(2)}) %collective-permute-start) | collective-permute-done | bytes 262176 | tf_op jit(solution)/shard_map/ppermute | solution.py:21
  51.9 3.5 %shard_map.69 = bf16[2,768,768]{2,1,0:T(8,128)(2,1)} custom-call(s32[2,72]{1,0:T(2,128)} %pad_add_fusion.table_ref, bf16[64,128,128]{2,1,0:T(8,128)(2,1)} %bitcast.112), custom_call_target="tpu_custom_call" | custom-call | bytes 4456448 | tf_op jit(solution)/shard_map/pallas_call | solution.py:77
  55.3 3.5 %fusion.9 = f32[2,512,768]{2,1,0:T(8,128)S(1)} fusion(bf16[2,768,768]{2,1,0:T(8,128)(2,1)} %shard_map.69, bf16[2,256,768]{2,1,0:T(8,128)(2,1)} %get-tuple-element.52, bf16[2,256,768]{2,1,0:T(8,128)(2,1)} %get-tuple-element.51), kind=kOutput, calls=%fused_computation.22 | convolution fusion | flops 1211105280 | bytes 7077888 | tf_op jit(solution)/shard_map/ncm,nmk->nck/dot_general | solution.py:187
  59.1 4.4 %collective-permute-start.2 = (f32[256,256]{1,0:T(8,128)S(1)}, f32[256,256]{1,0:T(8,128)S(1)}, u32[]{:S(2)}, u32[]{:S(2)}) collective-permute-start(f32[256,256]{1,0:T(8,128)S(1)} %get-tuple-element.46), channel_id=1, source_target_pairs={{4,0},{8,4},{12,8},{16,12},{20,16},{24,20},{28,24},{32,28},{36,32}... | collective-permute-start | bytes 786440 | tf_op jit(solution)/shard_map/ppermute | solution.py:21
  63.6 3.6 %collective-permute-start.5 = (f32[2,256,128]{2,1,0:T(8,128)S(1)}, f32[2,256,128]{2,1,0:T(8,128)S(1)}, u32[]{:S(2)}, u32[]{:S(2)}) collective-permute-start(f32[2,256,128]{2,1,0:T(8,128)S(1)} %get-tuple-element.49), channel_id=1, source_target_pairs={{0,1},{1,2},{2,3},{4,5},{5,6},{6,7},{8,9},{9,10},{10,11},{12,13},{... | collective-permute-start | bytes 786440 | tf_op jit(solution)/shard_map/ppermute | solution.py:21
  68.4 2.1 %collective-permute-start.4 = (f32[256,256]{1,0:T(8,128)S(1)}, f32[256,256]{1,0:T(8,128)S(1)}, u32[]{:S(2)}, u32[]{:S(2)}) collective-permute-start(f32[256,256]{1,0:T(8,128)S(1)} %get-tuple-element.45), channel_id=1, source_target_pairs={{0,4},{4,8},{8,12},{12,16},{16,20},{20,24},{24,28},{28,32},{32,36}... | collective-permute-start | bytes 786440 | tf_op jit(solution)/shard_map/ppermute | solution.py:21
  70.6 2.1 %collective-permute-done.5 = f32[2,256,128]{2,1,0:T(8,128)S(1)} collective-permute-done((f32[2,256,128]{2,1,0:T(8,128)S(1)}, f32[2,256,128]{2,1,0:T(8,128)S(1)}, u32[]{:S(2)}, u32[]{:S(2)}) %collective-permute-start.5) | collective-permute-done | bytes 262176 | tf_op jit(solution)/shard_map/ppermute | solution.py:21
  72.7 4.2 %collective-permute-done.3 = f32[2,256,128]{2,1,0:T(8,128)S(1)} collective-permute-done((f32[2,256,128]{2,1,0:T(8,128)S(1)}, f32[2,256,128]{2,1,0:T(8,128)S(1)}, u32[]{:S(2)}, u32[]{:S(2)}) %collective-permute-start.3) | collective-permute-done | bytes 262176 | tf_op jit(solution)/shard_map/ppermute | solution.py:21
  77.6 1.4 %copy-done.2 = bf16[2,768,768]{2,1,0:T(8,128)(2,1)S(1)} copy-done((bf16[2,768,768]{2,1,0:T(8,128)(2,1)S(1)}, bf16[2,768,768]{2,1,0:T(8,128)(2,1)}, u32[]{:S(2)}) %copy-start.2) | copy-done | bytes 2359320
  80.7 3.1 %collective-permute-start.6 = (f32[256,256]{1,0:T(8,128)S(1)}, f32[256,256]{1,0:T(8,128)S(1)}, u32[]{:S(2)}, u32[]{:S(2)}) collective-permute-start(f32[256,256]{1,0:T(8,128)S(1)} %get-tuple-element.38), channel_id=1, source_target_pairs={{4,0},{8,4},{12,8},{16,12},{20,16},{24,20},{28,24},{32,28},{36,32}... | collective-permute-start | bytes 786440 | tf_op jit(solution)/shard_map/ppermute | solution.py:21
  83.9 4.3 %collective-permute-start.9 = (f32[2,256,128]{2,1,0:T(8,128)S(1)}, f32[2,256,128]{2,1,0:T(8,128)S(1)}, u32[]{:S(2)}, u32[]{:S(2)}) collective-permute-start(f32[2,256,128]{2,1,0:T(8,128)S(1)} %get-tuple-element.41), channel_id=1, source_target_pairs={{0,1},{1,2},{2,3},{4,5},{5,6},{6,7},{8,9},{9,10},{10,11},{12,13},{... | collective-permute-start | bytes 786440 | tf_op jit(solution)/shard_map/ppermute | solution.py:21
  89.5 1.9 %collective-permute-start.8 = (f32[256,256]{1,0:T(8,128)S(1)}, f32[256,256]{1,0:T(8,128)S(1)}, u32[]{:S(2)}, u32[]{:S(2)}) collective-permute-start(f32[256,256]{1,0:T(8,128)S(1)} %get-tuple-element.37), channel_id=1, source_target_pairs={{0,4},{4,8},{8,12},{12,16},{16,20},{20,24},{24,28},{28,32},{32,36}... | collective-permute-start | bytes 786440 | tf_op jit(solution)/shard_map/ppermute | solution.py:21
  91.5 1.8 %collective-permute-done.9 = f32[2,256,128]{2,1,0:T(8,128)S(1)} collective-permute-done((f32[2,256,128]{2,1,0:T(8,128)S(1)}, f32[2,256,128]{2,1,0:T(8,128)S(1)}, u32[]{:S(2)}, u32[]{:S(2)}) %collective-permute-start.9) | collective-permute-done | bytes 262176 | tf_op jit(solution)/shard_map/ppermute | solution.py:21
  93.3 4.2 %collective-permute-done.7 = f32[2,256,128]{2,1,0:T(8,128)S(1)} collective-permute-done((f32[2,256,128]{2,1,0:T(8,128)S(1)}, f32[2,256,128]{2,1,0:T(8,128)S(1)}, u32[]{:S(2)}, u32[]{:S(2)}) %collective-permute-start.7) | collective-permute-done | bytes 262176 | tf_op jit(solution)/shard_map/ppermute | solution.py:21
  100.0 4.1 %collective-permute-start.10 = (f32[256,256]{1,0:T(8,128)S(1)}, f32[256,256]{1,0:T(8,128)S(1)}, u32[]{:S(2)}, u32[]{:S(2)}) collective-permute-start(f32[256,256]{1,0:T(8,128)S(1)} %get-tuple-element.29), channel_id=1, source_target_pairs={{4,0},{8,4},{12,8},{16,12},{20,16},{24,20},{28,24},{32,28},{36,32}... | collective-permute-start | bytes 786440 | tf_op jit(solution)/shard_map/ppermute | solution.py:21
  104.2 4.3 %collective-permute-start.13 = (f32[2,256,128]{2,1,0:T(8,128)S(1)}, f32[2,256,128]{2,1,0:T(8,128)S(1)}, u32[]{:S(2)}, u32[]{:S(2)}) collective-permute-start(f32[2,256,128]{2,1,0:T(8,128)S(1)} %get-tuple-element.33), channel_id=1, source_target_pairs={{0,1},{1,2},{2,3},{4,5},{5,6},{6,7},{8,9},{9,10},{10,11},{12,13},{... | collective-permute-start | bytes 786440 | tf_op jit(solution)/shard_map/ppermute | solution.py:21
  109.8 2.1 %collective-permute-start.12 = (f32[256,256]{1,0:T(8,128)S(1)}, f32[256,256]{1,0:T(8,128)S(1)}, u32[]{:S(2)}, u32[]{:S(2)}) collective-permute-start(f32[256,256]{1,0:T(8,128)S(1)} %get-tuple-element.28), channel_id=1, source_target_pairs={{0,4},{4,8},{8,12},{12,16},{16,20},{20,24},{24,28},{28,32},{32,36}... | collective-permute-start | bytes 786440 | tf_op jit(solution)/shard_map/ppermute | solution.py:21
  112.0 2.0 %collective-permute-done.13 = f32[2,256,128]{2,1,0:T(8,128)S(1)} collective-permute-done((f32[2,256,128]{2,1,0:T(8,128)S(1)}, f32[2,256,128]{2,1,0:T(8,128)S(1)}, u32[]{:S(2)}, u32[]{:S(2)}) %collective-permute-start.13) | collective-permute-done | bytes 262176 | tf_op jit(solution)/shard_map/ppermute | solution.py:21
  114.1 3.8 %collective-permute-done.11 = f32[2,256,128]{2,1,0:T(8,128)S(1)} collective-permute-done((f32[2,256,128]{2,1,0:T(8,128)S(1)}, f32[2,256,128]{2,1,0:T(8,128)S(1)}, u32[]{:S(2)}, u32[]{:S(2)}) %collective-permute-start.11) | collective-permute-done | bytes 262176 | tf_op jit(solution)/shard_map/ppermute | solution.py:21
  120.5 3.3 %collective-permute-start.14 = (f32[256,256]{1,0:T(8,128)S(1)}, f32[256,256]{1,0:T(8,128)S(1)}, u32[]{:S(2)}, u32[]{:S(2)}) collective-permute-start(f32[256,256]{1,0:T(8,128)S(1)} %get-tuple-element.25), channel_id=1, source_target_pairs={{4,0},{8,4},{12,8},{16,12},{20,16},{24,20},{28,24},{32,28},{36,32}... | collective-permute-start | bytes 786440 | tf_op jit(solution)/shard_map/ppermute | solution.py:21
  125.3 2.9 %collective-permute-done.14 = f32[256,256]{1,0:T(8,128)S(1)} collective-permute-done((f32[256,256]{1,0:T(8,128)S(1)}, f32[256,256]{1,0:T(8,128)S(1)}, u32[]{:S(2)}, u32[]{:S(2)}) %collective-permute-start.14) | collective-permute-done | bytes 262176 | tf_op jit(solution)/shard_map/ppermute | solution.py:21
  128.2 6.6 %collective-permute-done.15 = f32[2,256,128]{2,1,0:T(8,128)S(1)} collective-permute-done((f32[2,256,128]{2,1,0:T(8,128)S(1)}, f32[2,256,128]{2,1,0:T(8,128)S(1)}, u32[]{:S(2)}, u32[]{:S(2)}) %collective-permute-start.15) | collective-permute-done | bytes 262176 | tf_op jit(solution)/shard_map/ppermute | solution.py:21
  134.9 1.6 %fusion.32 = (f32[2,1,256,384]{3,2,1,0:T(8,128)}, f32[2,1,256,384]{3,2,1,0:T(8,128)}) fusion(f32[2,1,256,128]{3,2,0,1:T(8,128)S(1)} %fusion.34, f32[2,1,256,256]{3,2,0,1:T(8,128)S(1)} %fusion.33, f32[2,1,256,128]{3,2,0,1:T(8,128)S(1)} %bitcast.117, f32[2,1,256,256]{3,2,0,1:T(8,128)S(1)} %fusion.61, f32[2,1,256,128]{3,2,0,1:T(8,128)S(1)} %bitcast.116, ...), kind=kLoop, calls=%fused_computation.51 | loop fusion | flops 4325376 | bytes 5508096
  (113 shorter events, 21.2 us)
Async XLA Ops:
  13.3 7.9 %copy-start.5 = (s32[64,1]{0,1:T(1,128)S(1)}, s32[64,1]{0,1:T(1,128)}, u32[]{:S(2)}) copy-start(s32[64,1]{0,1:T(1,128)} %param.5) | copy-start | bytes 772
  13.3 37.2 %all-to-all-start = ((bf16[32,256,128]{2,1,0:T(8,128)(2,1)}), bf16[32,256,128]{2,1,0:T(8,128)(2,1)S(1)}, u32[]{:S(2)}, u32[]{:S(2)}) async-start(bf16[32,256,128]{2,1,0:T(8,128)(2,1)} %bitcast.113), calls=%async_computation | async-start | bytes 4194304 | tf_op jit(solution)/shard_map/all_to_all | solution.py:149
  24.0 14.2 %copy-start.6 = (s32[6]{0:T(128)S(1)}, s32[6]{0:T(128)}, u32[]{:S(2)}) copy-start(s32[6]{0:T(128)} %constant.128.clone) | copy-start | bytes 76
  24.7 23.4 %collective-permute-start = (f32[256,256]{1,0:T(8,128)}, f32[256,256]{1,0:T(8,128)S(1)}, u32[]{:S(2)}, u32[]{:S(2)}) collective-permute-start(f32[256,256]{1,0:T(8,128)} %slice_bitcast_fusion.7), channel_id=1, source_target_pairs={{0,4},{4,8},{8,12},{12,16},{16,20},{20,24},{24,28},{28,32},{32,36}... | collective-permute-start | bytes 786440 | tf_op jit(solution)/shard_map/ppermute | solution.py:21
  28.8 20.3 %collective-permute-start.1 = (f32[2,256,128]{2,1,0:T(8,128)}, f32[2,256,128]{2,1,0:T(8,128)S(1)}, u32[]{:S(2)}, u32[]{:S(2)}) collective-permute-start(f32[2,256,128]{2,1,0:T(8,128)} %slice.225), channel_id=1, source_target_pairs={{0,1},{1,2},{2,3},{4,5},{5,6},{6,7},{8,9},{9,10},{10,11},{12,13},{... | collective-permute-start | bytes 786440 | tf_op jit(solution)/shard_map/ppermute | solution.py:21
  39.0 10.1 %copy-start.3 = (f32[2,256,256]{2,1,0:T(8,128)S(1)}, f32[2,256,256]{2,1,0:T(8,128)}, u32[]{:S(2)}) copy-start(f32[2,256,256]{2,1,0:T(8,128)} %slice.224) | copy-start | bytes 1572868
  39.1 10.1 %copy-start.4 = (f32[2,256,128]{2,1,0:T(8,128)S(1)}, f32[2,256,128]{2,1,0:T(8,128)}, u32[]{:S(2)}) copy-start(f32[2,256,128]{2,1,0:T(8,128)} %slice.226) | copy-start | bytes 786436
  50.5 1.4 copy-start
  59.1 11.4 %collective-permute-start.2 = (f32[256,256]{1,0:T(8,128)S(1)}, f32[256,256]{1,0:T(8,128)S(1)}, u32[]{:S(2)}, u32[]{:S(2)}) collective-permute-start(f32[256,256]{1,0:T(8,128)S(1)} %get-tuple-element.46), channel_id=1, source_target_pairs={{4,0},{8,4},{12,8},{16,12},{20,16},{24,20},{28,24},{32,28},{36,32}... | collective-permute-start | bytes 786440 | tf_op jit(solution)/shard_map/ppermute | solution.py:21
  63.6 9.2 %collective-permute-start.5 = (f32[2,256,128]{2,1,0:T(8,128)S(1)}, f32[2,256,128]{2,1,0:T(8,128)S(1)}, u32[]{:S(2)}, u32[]{:S(2)}) collective-permute-start(f32[2,256,128]{2,1,0:T(8,128)S(1)} %get-tuple-element.49), channel_id=1, source_target_pairs={{0,1},{1,2},{2,3},{4,5},{5,6},{6,7},{8,9},{9,10},{10,11},{12,13},{... | collective-permute-start | bytes 786440 | tf_op jit(solution)/shard_map/ppermute | solution.py:21
  67.1 9.8 %collective-permute-start.3 = (f32[2,256,128]{2,1,0:T(8,128)S(1)}, f32[2,256,128]{2,1,0:T(8,128)S(1)}, u32[]{:S(2)}, u32[]{:S(2)}) collective-permute-start(f32[2,256,128]{2,1,0:T(8,128)S(1)} %get-tuple-element.50), channel_id=1, source_target_pairs={{1,0},{2,1},{3,2},{5,4},{6,5},{7,6},{9,8},{10,9},{11,10},{13,12},{... | collective-permute-start | bytes 786440 | tf_op jit(solution)/shard_map/ppermute | solution.py:21
  68.4 8.8 %collective-permute-start.4 = (f32[256,256]{1,0:T(8,128)S(1)}, f32[256,256]{1,0:T(8,128)S(1)}, u32[]{:S(2)}, u32[]{:S(2)}) collective-permute-start(f32[256,256]{1,0:T(8,128)S(1)} %get-tuple-element.45), channel_id=1, source_target_pairs={{0,4},{4,8},{8,12},{12,16},{16,20},{20,24},{24,28},{28,32},{32,36}... | collective-permute-start | bytes 786440 | tf_op jit(solution)/shard_map/ppermute | solution.py:21
  77.4 1.7 %copy-start.2 = (bf16[2,768,768]{2,1,0:T(8,128)(2,1)S(1)}, bf16[2,768,768]{2,1,0:T(8,128)(2,1)}, u32[]{:S(2)}) copy-start(bf16[2,768,768]{2,1,0:T(8,128)(2,1)} %shard_map.69) | copy-start | bytes 7077892
  80.7 10.7 %collective-permute-start.6 = (f32[256,256]{1,0:T(8,128)S(1)}, f32[256,256]{1,0:T(8,128)S(1)}, u32[]{:S(2)}, u32[]{:S(2)}) collective-permute-start(f32[256,256]{1,0:T(8,128)S(1)} %get-tuple-element.38), channel_id=1, source_target_pairs={{4,0},{8,4},{12,8},{16,12},{20,16},{24,20},{28,24},{32,28},{36,32}... | collective-permute-start | bytes 786440 | tf_op jit(solution)/shard_map/ppermute | solution.py:21
  83.9 9.4 %collective-permute-start.9 = (f32[2,256,128]{2,1,0:T(8,128)S(1)}, f32[2,256,128]{2,1,0:T(8,128)S(1)}, u32[]{:S(2)}, u32[]{:S(2)}) collective-permute-start(f32[2,256,128]{2,1,0:T(8,128)S(1)} %get-tuple-element.41), channel_id=1, source_target_pairs={{0,1},{1,2},{2,3},{4,5},{5,6},{6,7},{8,9},{9,10},{10,11},{12,13},{... | collective-permute-start | bytes 786440 | tf_op jit(solution)/shard_map/ppermute | solution.py:21
  88.2 9.2 %collective-permute-start.7 = (f32[2,256,128]{2,1,0:T(8,128)S(1)}, f32[2,256,128]{2,1,0:T(8,128)S(1)}, u32[]{:S(2)}, u32[]{:S(2)}) collective-permute-start(f32[2,256,128]{2,1,0:T(8,128)S(1)} %get-tuple-element.42), channel_id=1, source_target_pairs={{1,0},{2,1},{3,2},{5,4},{6,5},{7,6},{9,8},{10,9},{11,10},{13,12},{... | collective-permute-start | bytes 786440 | tf_op jit(solution)/shard_map/ppermute | solution.py:21
  89.5 8.4 %collective-permute-start.8 = (f32[256,256]{1,0:T(8,128)S(1)}, f32[256,256]{1,0:T(8,128)S(1)}, u32[]{:S(2)}, u32[]{:S(2)}) collective-permute-start(f32[256,256]{1,0:T(8,128)S(1)} %get-tuple-element.37), channel_id=1, source_target_pairs={{0,4},{4,8},{8,12},{12,16},{16,20},{20,24},{24,28},{28,32},{32,36}... | collective-permute-start | bytes 786440 | tf_op jit(solution)/shard_map/ppermute | solution.py:21
  100.0 12.0 %collective-permute-start.10 = (f32[256,256]{1,0:T(8,128)S(1)}, f32[256,256]{1,0:T(8,128)S(1)}, u32[]{:S(2)}, u32[]{:S(2)}) collective-permute-start(f32[256,256]{1,0:T(8,128)S(1)} %get-tuple-element.29), channel_id=1, source_target_pairs={{4,0},{8,4},{12,8},{16,12},{20,16},{24,20},{28,24},{32,28},{36,32}... | collective-permute-start | bytes 786440 | tf_op jit(solution)/shard_map/ppermute | solution.py:21
  104.2 9.9 %collective-permute-start.13 = (f32[2,256,128]{2,1,0:T(8,128)S(1)}, f32[2,256,128]{2,1,0:T(8,128)S(1)}, u32[]{:S(2)}, u32[]{:S(2)}) collective-permute-start(f32[2,256,128]{2,1,0:T(8,128)S(1)} %get-tuple-element.33), channel_id=1, source_target_pairs={{0,1},{1,2},{2,3},{4,5},{5,6},{6,7},{8,9},{9,10},{10,11},{12,13},{... | collective-permute-start | bytes 786440 | tf_op jit(solution)/shard_map/ppermute | solution.py:21
  108.4 9.5 %collective-permute-start.11 = (f32[2,256,128]{2,1,0:T(8,128)S(1)}, f32[2,256,128]{2,1,0:T(8,128)S(1)}, u32[]{:S(2)}, u32[]{:S(2)}) collective-permute-start(f32[2,256,128]{2,1,0:T(8,128)S(1)} %get-tuple-element.34), channel_id=1, source_target_pairs={{1,0},{2,1},{3,2},{5,4},{6,5},{7,6},{9,8},{10,9},{11,10},{13,12},{... | collective-permute-start | bytes 786440 | tf_op jit(solution)/shard_map/ppermute | solution.py:21
  109.8 8.7 %collective-permute-start.12 = (f32[256,256]{1,0:T(8,128)S(1)}, f32[256,256]{1,0:T(8,128)S(1)}, u32[]{:S(2)}, u32[]{:S(2)}) collective-permute-start(f32[256,256]{1,0:T(8,128)S(1)} %get-tuple-element.28), channel_id=1, source_target_pairs={{0,4},{4,8},{8,12},{12,16},{16,20},{20,24},{24,28},{28,32},{32,36}... | collective-permute-start | bytes 786440 | tf_op jit(solution)/shard_map/ppermute | solution.py:21
  120.5 7.7 %collective-permute-start.14 = (f32[256,256]{1,0:T(8,128)S(1)}, f32[256,256]{1,0:T(8,128)S(1)}, u32[]{:S(2)}, u32[]{:S(2)}) collective-permute-start(f32[256,256]{1,0:T(8,128)S(1)} %get-tuple-element.25), channel_id=1, source_target_pairs={{4,0},{8,4},{12,8},{16,12},{20,16},{24,20},{28,24},{32,28},{36,32}... | collective-permute-start | bytes 786440 | tf_op jit(solution)/shard_map/ppermute | solution.py:21
  123.9 10.9 %collective-permute-start.15 = (f32[2,256,128]{2,1,0:T(8,128)S(1)}, f32[2,256,128]{2,1,0:T(8,128)S(1)}, u32[]{:S(2)}, u32[]{:S(2)}) collective-permute-start(f32[2,256,128]{2,1,0:T(8,128)S(1)} %slice.266), channel_id=1, source_target_pairs={{1,0},{2,1},{3,2},{5,4},{6,5},{7,6},{9,8},{10,9},{11,10},{13,12},{... | collective-permute-start | bytes 786440 | tf_op jit(solution)/shard_map/ppermute | solution.py:21
  125.3 9.6 %copy-start.1 = (f32[2,1,256,384]{3,2,1,0:T(8,128)S(1)}, f32[2,1,256,384]{3,2,1,0:T(8,128)}, u32[]{:S(2)}) copy-start(f32[2,1,256,384]{3,2,1,0:T(8,128)} %param.8) | copy-start | bytes 2359300

commit v3 on v2

--- a/solution.py
+++ b/solution.py
@@ -22,7 +22,6 @@
 
 
 def _pack_kernel(code_ref, tiles_ref, out_ref, *, per_owner, owner_subs, block_len):
-    out_ref[...] = jnp.zeros_like(out_ref)
     previous = jnp.int32(-1)
     rank = jnp.int32(0)
     for j in range(tiles_ref.shape[0]):
@@ -66,7 +65,7 @@
                 out_ref[s, p * block_len : (p + 1) * block_len, q * block_len : (q + 1) * block_len] = tile
                 if q > p:
                     out_ref[s, q * block_len : (q + 1) * block_len, p * block_len : (p + 1) * block_len] = (
-                        tile.astype(jnp.float32).T.astype(tile.dtype)
+                        tile.T
                     )
 
 

time: 137 us -> 137 us (level)
  no operation moved by 1% of the time
where the time goes in v3:
time: 137 us; the launch traced here: 136 us
  starting transfers between devices  53.1 us (39%)
  waiting for transfers between devices  36 us (26%)
  matrix products  17.2 us (13%)
  local copies, waits for them, and re-layouts  11.4 us (8%)
  other arithmetic  10.9 us (8%)
  Pallas kernels  6.37 us (5%)
    ppermute x16, starting transfers between devices, from_behind(): lax.ppermute(value, axis, [(source, source + steps) for source in range(i...  45.3 us
    ppermute x16, waiting for transfers between devices, from_behind(): lax.ppermute(value, axis, [(source, source + steps) for source in range(i...  36 us
    dot_general x1, matrix products, shards(): jnp.einsum('jka,jkb->jab', factor_panels[:, 0, 0], factor_panels[:, 0, 1]...  9.51 us
    all_to_all x1, starting transfers between devices, shards(): lax.all_to_all(send_tiles, 'gx', split_axis=0, concat_axis=0, tiled=True)  7.85 us
    dot_general x4, matrix products, shards(): jnp.einsum('ncm,nmk->nck', jnp.concatenate([high, low], axis=1), matrices...  7.7 us
    pallas_call x1, Pallas kernels, matrix_tiles(): pl.pallas_call(partial(_matrix_kernel, subs=subs, blocks=blocks, block_le...  3.5 us
    pallas_call x1, Pallas kernels, pack_tiles(): pl.pallas_call(partial(_pack_kernel, per_owner=per_owner, owner_subs=owne...  2.88 us
    unnamed x14, local copies, waits for them, and re-layouts  2.8 us
  transfers between devices with their start and end apart: 17, of which 9 were waited for; matrix products, arithmetic and copies ran while one was open for 12% of the time, Pallas kernels for 0%

profile of v3, /device:TPU:17, one launch (start us, length us, event | category | flops | bytes accessed | tf_op | source)
XLA Modules:
  0.0 136.3 jit_solution(12516034995087541023)
XLA Ops:
  0.6 9.5 %fusion.25.tiles_ref = bf16[26,128,128]{2,1,0:T(8,128)(2,1)} fusion(bf16[26,1,2,1536,128]{4,3,2,1,0:T(8,128)(2,1)} %param.7), kind=kOutput, calls=%fused_computation.41 | convolution fusion | flops 1309048832 | bytes 21299200 | tf_op jit(solution)/shard_map/jka,jkb->jab/dot_general | solution.py:138
  10.1 2.9 %shard_map.68 = bf16[8192,128]{1,0:T(8,128)(2,1)} custom-call(s32[26]{0:T(128)} %bitcast.127, bf16[26,128,128]{2,1,0:T(8,128)(2,1)} %fusion.25.tiles_ref), custom_call_target="tpu_custom_call" | custom-call | bytes 2949120 | tf_op jit(solution)/shard_map/pallas_call | solution.py:43
  13.0 7.8 %all-to-all-start = ((bf16[32,256,128]{2,1,0:T(8,128)(2,1)}), bf16[32,256,128]{2,1,0:T(8,128)(2,1)S(1)}, u32[]{:S(2)}, u32[]{:S(2)}) async-start(bf16[32,256,128]{2,1,0:T(8,128)(2,1)} %bitcast.113), calls=%async_computation | async-start | bytes 4194304 | tf_op jit(solution)/shard_map/all_to_all | solution.py:148
  21.6 2.1 %broadcast_multiply_fusion = (f32[2,256,384]{2,1,0:T(8,128)}, f32[2,256,384]{2,1,0:T(8,128)S(1)}) fusion(f32[2,384]{1,0:T(2,128)S(1)} %pad_convert_fusion, f32[2,1,256,384]{3,2,1,0:T(8,128)} %param.8), kind=kLoop, calls=%fused_computation.66 | loop fusion | flops 393216 | bytes 2362368 | tf_op jit(solution)/shard_map/div | solution.py:173
  24.4 3.4 %collective-permute-start = (f32[256,256]{1,0:T(8,128)}, f32[256,256]{1,0:T(8,128)S(1)}, u32[]{:S(2)}, u32[]{:S(2)}) collective-permute-start(f32[256,256]{1,0:T(8,128)} %slice_bitcast_fusion.7), channel_id=1, source_target_pairs={{0,4},{4,8},{8,12},{12,16},{16,20},{20,24},{24,28},{28,32},{32,36}... | collective-permute-start | bytes 786440 | tf_op jit(solution)/shard_map/ppermute | solution.py:21
  28.5 3.5 %collective-permute-start.1 = (f32[2,256,128]{2,1,0:T(8,128)}, f32[2,256,128]{2,1,0:T(8,128)S(1)}, u32[]{:S(2)}, u32[]{:S(2)}) collective-permute-start(f32[2,256,128]{2,1,0:T(8,128)} %slice.225), channel_id=1, source_target_pairs={{0,1},{1,2},{2,3},{4,5},{5,6},{6,7},{8,9},{9,10},{10,11},{12,13},{... | collective-permute-start | bytes 786440 | tf_op jit(solution)/shard_map/ppermute | solution.py:21
  32.2 1.7 %slice.226 = f32[2,256,128]{2,1,0:T(8,128)} slice(f32[2,256,384]{2,1,0:T(8,128)} %get-tuple-element.14), slice={[0:2], [0:256], [256:384]} | slice | bytes 524288 | tf_op jit(solution)/shard_map/slice | solution.py:180
  33.8 1.7 %slice.223 = f32[1,256,256]{2,1,0:T(8,128)} slice(f32[2,256,384]{2,1,0:T(8,128)} %get-tuple-element.14), slice={[0:1], [0:256], [0:256]} | slice | bytes 524288 | tf_op jit(solution)/shard_map/slice | solution.py:181
  35.5 1.9 %slice.224 = f32[2,256,256]{2,1,0:T(8,128)} slice(f32[2,256,384]{2,1,0:T(8,128)} %get-tuple-element.14), slice={[0:2], [0:256], [0:256]} | slice | bytes 1048576 | tf_op jit(solution)/shard_map/slice | solution.py:179
  39.5 8.3 %collective-permute-done = f32[256,256]{1,0:T(8,128)S(1)} collective-permute-done((f32[256,256]{1,0:T(8,128)}, f32[256,256]{1,0:T(8,128)S(1)}, u32[]{:S(2)}, u32[]{:S(2)}) %collective-permute-start) | collective-permute-done | bytes 262176 | tf_op jit(solution)/shard_map/ppermute | solution.py:21
  51.6 3.5 %shard_map.69 = bf16[2,768,768]{2,1,0:T(8,128)(2,1)} custom-call(s32[2,72]{1,0:T(2,128)} %pad_add_fusion.table_ref, bf16[64,128,128]{2,1,0:T(8,128)(2,1)} %bitcast.112), custom_call_target="tpu_custom_call" | custom-call | bytes 4456448 | tf_op jit(solution)/shard_map/pallas_call | solution.py:76
  55.1 3.5 %fusion.9 = f32[2,512,768]{2,1,0:T(8,128)S(1)} fusion(bf16[2,768,768]{2,1,0:T(8,128)(2,1)} %shard_map.69, bf16[2,256,768]{2,1,0:T(8,128)(2,1)} %get-tuple-element.52, bf16[2,256,768]{2,1,0:T(8,128)(2,1)} %get-tuple-element.51), kind=kOutput, calls=%fused_computation.22 | convolution fusion | flops 1211105280 | bytes 7077888 | tf_op jit(solution)/shard_map/ncm,nmk->nck/dot_general | solution.py:186
  58.9 4.4 %collective-permute-start.2 = (f32[256,256]{1,0:T(8,128)S(1)}, f32[256,256]{1,0:T(8,128)S(1)}, u32[]{:S(2)}, u32[]{:S(2)}) collective-permute-start(f32[256,256]{1,0:T(8,128)S(1)} %get-tuple-element.46), channel_id=1, source_target_pairs={{4,0},{8,4},{12,8},{16,12},{20,16},{24,20},{28,24},{32,28},{36,32}... | collective-permute-start | bytes 786440 | tf_op jit(solution)/shard_map/ppermute | solution.py:21
  63.3 3.6 %collective-permute-start.5 = (f32[2,256,128]{2,1,0:T(8,128)S(1)}, f32[2,256,128]{2,1,0:T(8,128)S(1)}, u32[]{:S(2)}, u32[]{:S(2)}) collective-permute-start(f32[2,256,128]{2,1,0:T(8,128)S(1)} %get-tuple-element.49), channel_id=1, source_target_pairs={{0,1},{1,2},{2,3},{4,5},{5,6},{6,7},{8,9},{9,10},{10,11},{12,13},{... | collective-permute-start | bytes 786440 | tf_op jit(solution)/shard_map/ppermute | solution.py:21
  68.2 2.1 %collective-permute-start.4 = (f32[256,256]{1,0:T(8,128)S(1)}, f32[256,256]{1,0:T(8,128)S(1)}, u32[]{:S(2)}, u32[]{:S(2)}) collective-permute-start(f32[256,256]{1,0:T(8,128)S(1)} %get-tuple-element.45), channel_id=1, source_target_pairs={{0,4},{4,8},{8,12},{12,16},{16,20},{20,24},{24,28},{28,32},{32,36}... | collective-permute-start | bytes 786440 | tf_op jit(solution)/shard_map/ppermute | solution.py:21
  70.4 2.1 %collective-permute-done.5 = f32[2,256,128]{2,1,0:T(8,128)S(1)} collective-permute-done((f32[2,256,128]{2,1,0:T(8,128)S(1)}, f32[2,256,128]{2,1,0:T(8,128)S(1)}, u32[]{:S(2)}, u32[]{:S(2)}) %collective-permute-start.5) | collective-permute-done | bytes 262176 | tf_op jit(solution)/shard_map/ppermute | solution.py:21
  72.5 4.2 %collective-permute-done.3 = f32[2,256,128]{2,1,0:T(8,128)S(1)} collective-permute-done((f32[2,256,128]{2,1,0:T(8,128)S(1)}, f32[2,256,128]{2,1,0:T(8,128)S(1)}, u32[]{:S(2)}, u32[]{:S(2)}) %collective-permute-start.3) | collective-permute-done | bytes 262176 | tf_op jit(solution)/shard_map/ppermute | solution.py:21
  77.4 1.4 %copy-done.2 = bf16[2,768,768]{2,1,0:T(8,128)(2,1)S(1)} copy-done((bf16[2,768,768]{2,1,0:T(8,128)(2,1)S(1)}, bf16[2,768,768]{2,1,0:T(8,128)(2,1)}, u32[]{:S(2)}) %copy-start.2) | copy-done | bytes 2359320
  80.5 3.1 %collective-permute-start.6 = (f32[256,256]{1,0:T(8,128)S(1)}, f32[256,256]{1,0:T(8,128)S(1)}, u32[]{:S(2)}, u32[]{:S(2)}) collective-permute-start(f32[256,256]{1,0:T(8,128)S(1)} %get-tuple-element.38), channel_id=1, source_target_pairs={{4,0},{8,4},{12,8},{16,12},{20,16},{24,20},{28,24},{32,28},{36,32}... | collective-permute-start | bytes 786440 | tf_op jit(solution)/shard_map/ppermute | solution.py:21
  83.7 4.3 %collective-permute-start.9 = (f32[2,256,128]{2,1,0:T(8,128)S(1)}, f32[2,256,128]{2,1,0:T(8,128)S(1)}, u32[]{:S(2)}, u32[]{:S(2)}) collective-permute-start(f32[2,256,128]{2,1,0:T(8,128)S(1)} %get-tuple-element.41), channel_id=1, source_target_pairs={{0,1},{1,2},{2,3},{4,5},{5,6},{6,7},{8,9},{9,10},{10,11},{12,13},{... | collective-permute-start | bytes 786440 | tf_op jit(solution)/shard_map/ppermute | solution.py:21
  89.3 1.9 %collective-permute-start.8 = (f32[256,256]{1,0:T(8,128)S(1)}, f32[256,256]{1,0:T(8,128)S(1)}, u32[]{:S(2)}, u32[]{:S(2)}) collective-permute-start(f32[256,256]{1,0:T(8,128)S(1)} %get-tuple-element.37), channel_id=1, source_target_pairs={{0,4},{4,8},{8,12},{12,16},{16,20},{20,24},{24,28},{28,32},{32,36}... | collective-permute-start | bytes 786440 | tf_op jit(solution)/shard_map/ppermute | solution.py:21
  91.3 1.8 %collective-permute-done.9 = f32[2,256,128]{2,1,0:T(8,128)S(1)} collective-permute-done((f32[2,256,128]{2,1,0:T(8,128)S(1)}, f32[2,256,128]{2,1,0:T(8,128)S(1)}, u32[]{:S(2)}, u32[]{:S(2)}) %collective-permute-start.9) | collective-permute-done | bytes 262176 | tf_op jit(solution)/shard_map/ppermute | solution.py:21
  93.1 4.2 %collective-permute-done.7 = f32[2,256,128]{2,1,0:T(8,128)S(1)} collective-permute-done((f32[2,256,128]{2,1,0:T(8,128)S(1)}, f32[2,256,128]{2,1,0:T(8,128)S(1)}, u32[]{:S(2)}, u32[]{:S(2)}) %collective-permute-start.7) | collective-permute-done | bytes 262176 | tf_op jit(solution)/shard_map/ppermute | solution.py:21
  99.8 4.1 %collective-permute-start.10 = (f32[256,256]{1,0:T(8,128)S(1)}, f32[256,256]{1,0:T(8,128)S(1)}, u32[]{:S(2)}, u32[]{:S(2)}) collective-permute-start(f32[256,256]{1,0:T(8,128)S(1)} %get-tuple-element.29), channel_id=1, source_target_pairs={{4,0},{8,4},{12,8},{16,12},{20,16},{24,20},{28,24},{32,28},{36,32}... | collective-permute-start | bytes 786440 | tf_op jit(solution)/shard_map/ppermute | solution.py:21
  103.9 4.3 %collective-permute-start.13 = (f32[2,256,128]{2,1,0:T(8,128)S(1)}, f32[2,256,128]{2,1,0:T(8,128)S(1)}, u32[]{:S(2)}, u32[]{:S(2)}) collective-permute-start(f32[2,256,128]{2,1,0:T(8,128)S(1)} %get-tuple-element.33), channel_id=1, source_target_pairs={{0,1},{1,2},{2,3},{4,5},{5,6},{6,7},{8,9},{9,10},{10,11},{12,13},{... | collective-permute-start | bytes 786440 | tf_op jit(solution)/shard_map/ppermute | solution.py:21
  109.6 2.1 %collective-permute-start.12 = (f32[256,256]{1,0:T(8,128)S(1)}, f32[256,256]{1,0:T(8,128)S(1)}, u32[]{:S(2)}, u32[]{:S(2)}) collective-permute-start(f32[256,256]{1,0:T(8,128)S(1)} %get-tuple-element.28), channel_id=1, source_target_pairs={{0,4},{4,8},{8,12},{12,16},{16,20},{20,24},{24,28},{28,32},{32,36}... | collective-permute-start | bytes 786440 | tf_op jit(solution)/shard_map/ppermute | solution.py:21
  111.8 2.0 %collective-permute-done.13 = f32[2,256,128]{2,1,0:T(8,128)S(1)} collective-permute-done((f32[2,256,128]{2,1,0:T(8,128)S(1)}, f32[2,256,128]{2,1,0:T(8,128)S(1)}, u32[]{:S(2)}, u32[]{:S(2)}) %collective-permute-start.13) | collective-permute-done | bytes 262176 | tf_op jit(solution)/shard_map/ppermute | solution.py:21
  113.8 3.8 %collective-permute-done.11 = f32[2,256,128]{2,1,0:T(8,128)S(1)} collective-permute-done((f32[2,256,128]{2,1,0:T(8,128)S(1)}, f32[2,256,128]{2,1,0:T(8,128)S(1)}, u32[]{:S(2)}, u32[]{:S(2)}) %collective-permute-start.11) | collective-permute-done | bytes 262176 | tf_op jit(solution)/shard_map/ppermute | solution.py:21
  120.2 3.3 %collective-permute-start.14 = (f32[256,256]{1,0:T(8,128)S(1)}, f32[256,256]{1,0:T(8,128)S(1)}, u32[]{:S(2)}, u32[]{:S(2)}) collective-permute-start(f32[256,256]{1,0:T(8,128)S(1)} %get-tuple-element.25), channel_id=1, source_target_pairs={{4,0},{8,4},{12,8},{16,12},{20,16},{24,20},{28,24},{32,28},{36,32}... | collective-permute-start | bytes 786440 | tf_op jit(solution)/shard_map/ppermute | solution.py:21
  125.1 2.9 %collective-permute-done.14 = f32[256,256]{1,0:T(8,128)S(1)} collective-permute-done((f32[256,256]{1,0:T(8,128)S(1)}, f32[256,256]{1,0:T(8,128)S(1)}, u32[]{:S(2)}, u32[]{:S(2)}) %collective-permute-start.14) | collective-permute-done | bytes 262176 | tf_op jit(solution)/shard_map/ppermute | solution.py:21
  128.0 6.6 %collective-permute-done.15 = f32[2,256,128]{2,1,0:T(8,128)S(1)} collective-permute-done((f32[2,256,128]{2,1,0:T(8,128)S(1)}, f32[2,256,128]{2,1,0:T(8,128)S(1)}, u32[]{:S(2)}, u32[]{:S(2)}) %collective-permute-start.15) | collective-permute-done | bytes 262176 | tf_op jit(solution)/shard_map/ppermute | solution.py:21
  134.7 1.6 %fusion.32 = (f32[2,1,256,384]{3,2,1,0:T(8,128)}, f32[2,1,256,384]{3,2,1,0:T(8,128)}) fusion(f32[2,1,256,128]{3,2,0,1:T(8,128)S(1)} %fusion.34, f32[2,1,256,256]{3,2,0,1:T(8,128)S(1)} %fusion.33, f32[2,1,256,128]{3,2,0,1:T(8,128)S(1)} %bitcast.117, f32[2,1,256,256]{3,2,0,1:T(8,128)S(1)} %fusion.61, f32[2,1,256,128]{3,2,0,1:T(8,128)S(1)} %bitcast.116, ...), kind=kLoop, calls=%fused_computation.51 | loop fusion | flops 4325376 | bytes 5508096
  (113 shorter events, 21.3 us)
Async XLA Ops:
  13.0 7.9 %copy-start.5 = (s32[64,1]{0,1:T(1,128)S(1)}, s32[64,1]{0,1:T(1,128)}, u32[]{:S(2)}) copy-start(s32[64,1]{0,1:T(1,128)} %param.5) | copy-start | bytes 772
  13.0 37.2 %all-to-all-start = ((bf16[32,256,128]{2,1,0:T(8,128)(2,1)}), bf16[32,256,128]{2,1,0:T(8,128)(2,1)S(1)}, u32[]{:S(2)}, u32[]{:S(2)}) async-start(bf16[32,256,128]{2,1,0:T(8,128)(2,1)} %bitcast.113), calls=%async_computation | async-start | bytes 4194304 | tf_op jit(solution)/shard_map/all_to_all | solution.py:148
  23.7 14.2 %copy-start.6 = (s32[6]{0:T(128)S(1)}, s32[6]{0:T(128)}, u32[]{:S(2)}) copy-start(s32[6]{0:T(128)} %constant.128.clone) | copy-start | bytes 76
  24.4 23.4 %collective-permute-start = (f32[256,256]{1,0:T(8,128)}, f32[256,256]{1,0:T(8,128)S(1)}, u32[]{:S(2)}, u32[]{:S(2)}) collective-permute-start(f32[256,256]{1,0:T(8,128)} %slice_bitcast_fusion.7), channel_id=1, source_target_pairs={{0,4},{4,8},{8,12},{12,16},{16,20},{20,24},{24,28},{28,32},{32,36}... | collective-permute-start | bytes 786440 | tf_op jit(solution)/shard_map/ppermute | solution.py:21
  28.5 20.3 %collective-permute-start.1 = (f32[2,256,128]{2,1,0:T(8,128)}, f32[2,256,128]{2,1,0:T(8,128)S(1)}, u32[]{:S(2)}, u32[]{:S(2)}) collective-permute-start(f32[2,256,128]{2,1,0:T(8,128)} %slice.225), channel_id=1, source_target_pairs={{0,1},{1,2},{2,3},{4,5},{5,6},{6,7},{8,9},{9,10},{10,11},{12,13},{... | collective-permute-start | bytes 786440 | tf_op jit(solution)/shard_map/ppermute | solution.py:21
  38.8 10.1 %copy-start.3 = (f32[2,256,256]{2,1,0:T(8,128)S(1)}, f32[2,256,256]{2,1,0:T(8,128)}, u32[]{:S(2)}) copy-start(f32[2,256,256]{2,1,0:T(8,128)} %slice.224) | copy-start | bytes 1572868
  38.8 10.1 %copy-start.4 = (f32[2,256,128]{2,1,0:T(8,128)S(1)}, f32[2,256,128]{2,1,0:T(8,128)}, u32[]{:S(2)}) copy-start(f32[2,256,128]{2,1,0:T(8,128)} %slice.226) | copy-start | bytes 786436
  50.2 1.4 copy-start
  58.9 11.4 %collective-permute-start.2 = (f32[256,256]{1,0:T(8,128)S(1)}, f32[256,256]{1,0:T(8,128)S(1)}, u32[]{:S(2)}, u32[]{:S(2)}) collective-permute-start(f32[256,256]{1,0:T(8,128)S(1)} %get-tuple-element.46), channel_id=1, source_target_pairs={{4,0},{8,4},{12,8},{16,12},{20,16},{24,20},{28,24},{32,28},{36,32}... | collective-permute-start | bytes 786440 | tf_op jit(solution)/shard_map/ppermute | solution.py:21
  63.3 9.2 %collective-permute-start.5 = (f32[2,256,128]{2,1,0:T(8,128)S(1)}, f32[2,256,128]{2,1,0:T(8,128)S(1)}, u32[]{:S(2)}, u32[]{:S(2)}) collective-permute-start(f32[2,256,128]{2,1,0:T(8,128)S(1)} %get-tuple-element.49), channel_id=1, source_target_pairs={{0,1},{1,2},{2,3},{4,5},{5,6},{6,7},{8,9},{9,10},{10,11},{12,13},{... | collective-permute-start | bytes 786440 | tf_op jit(solution)/shard_map/ppermute | solution.py:21
  66.9 9.8 %collective-permute-start.3 = (f32[2,256,128]{2,1,0:T(8,128)S(1)}, f32[2,256,128]{2,1,0:T(8,128)S(1)}, u32[]{:S(2)}, u32[]{:S(2)}) collective-permute-start(f32[2,256,128]{2,1,0:T(8,128)S(1)} %get-tuple-element.50), channel_id=1, source_target_pairs={{1,0},{2,1},{3,2},{5,4},{6,5},{7,6},{9,8},{10,9},{11,10},{13,12},{... | collective-permute-start | bytes 786440 | tf_op jit(solution)/shard_map/ppermute | solution.py:21
  68.2 8.8 %collective-permute-start.4 = (f32[256,256]{1,0:T(8,128)S(1)}, f32[256,256]{1,0:T(8,128)S(1)}, u32[]{:S(2)}, u32[]{:S(2)}) collective-permute-start(f32[256,256]{1,0:T(8,128)S(1)} %get-tuple-element.45), channel_id=1, source_target_pairs={{0,4},{4,8},{8,12},{12,16},{16,20},{20,24},{24,28},{28,32},{32,36}... | collective-permute-start | bytes 786440 | tf_op jit(solution)/shard_map/ppermute | solution.py:21
  77.2 1.7 %copy-start.2 = (bf16[2,768,768]{2,1,0:T(8,128)(2,1)S(1)}, bf16[2,768,768]{2,1,0:T(8,128)(2,1)}, u32[]{:S(2)}) copy-start(bf16[2,768,768]{2,1,0:T(8,128)(2,1)} %shard_map.69) | copy-start | bytes 7077892
  80.5 10.7 %collective-permute-start.6 = (f32[256,256]{1,0:T(8,128)S(1)}, f32[256,256]{1,0:T(8,128)S(1)}, u32[]{:S(2)}, u32[]{:S(2)}) collective-permute-start(f32[256,256]{1,0:T(8,128)S(1)} %get-tuple-element.38), channel_id=1, source_target_pairs={{4,0},{8,4},{12,8},{16,12},{20,16},{24,20},{28,24},{32,28},{36,32}... | collective-permute-start | bytes 786440 | tf_op jit(solution)/shard_map/ppermute | solution.py:21
  83.7 9.4 %collective-permute-start.9 = (f32[2,256,128]{2,1,0:T(8,128)S(1)}, f32[2,256,128]{2,1,0:T(8,128)S(1)}, u32[]{:S(2)}, u32[]{:S(2)}) collective-permute-start(f32[2,256,128]{2,1,0:T(8,128)S(1)} %get-tuple-element.41), channel_id=1, source_target_pairs={{0,1},{1,2},{2,3},{4,5},{5,6},{6,7},{8,9},{9,10},{10,11},{12,13},{... | collective-permute-start | bytes 786440 | tf_op jit(solution)/shard_map/ppermute | solution.py:21
  88.0 9.2 %collective-permute-start.7 = (f32[2,256,128]{2,1,0:T(8,128)S(1)}, f32[2,256,128]{2,1,0:T(8,128)S(1)}, u32[]{:S(2)}, u32[]{:S(2)}) collective-permute-start(f32[2,256,128]{2,1,0:T(8,128)S(1)} %get-tuple-element.42), channel_id=1, source_target_pairs={{1,0},{2,1},{3,2},{5,4},{6,5},{7,6},{9,8},{10,9},{11,10},{13,12},{... | collective-permute-start | bytes 786440 | tf_op jit(solution)/shard_map/ppermute | solution.py:21
  89.3 8.4 %collective-permute-start.8 = (f32[256,256]{1,0:T(8,128)S(1)}, f32[256,256]{1,0:T(8,128)S(1)}, u32[]{:S(2)}, u32[]{:S(2)}) collective-permute-start(f32[256,256]{1,0:T(8,128)S(1)} %get-tuple-element.37), channel_id=1, source_target_pairs={{0,4},{4,8},{8,12},{12,16},{16,20},{20,24},{24,28},{28,32},{32,36}... | collective-permute-start | bytes 786440 | tf_op jit(solution)/shard_map/ppermute | solution.py:21
  99.8 12.0 %collective-permute-start.10 = (f32[256,256]{1,0:T(8,128)S(1)}, f32[256,256]{1,0:T(8,128)S(1)}, u32[]{:S(2)}, u32[]{:S(2)}) collective-permute-start(f32[256,256]{1,0:T(8,128)S(1)} %get-tuple-element.29), channel_id=1, source_target_pairs={{4,0},{8,4},{12,8},{16,12},{20,16},{24,20},{28,24},{32,28},{36,32}... | collective-permute-start | bytes 786440 | tf_op jit(solution)/shard_map/ppermute | solution.py:21
  103.9 9.9 %collective-permute-start.13 = (f32[2,256,128]{2,1,0:T(8,128)S(1)}, f32[2,256,128]{2,1,0:T(8,128)S(1)}, u32[]{:S(2)}, u32[]{:S(2)}) collective-permute-start(f32[2,256,128]{2,1,0:T(8,128)S(1)} %get-tuple-element.33), channel_id=1, source_target_pairs={{0,1},{1,2},{2,3},{4,5},{5,6},{6,7},{8,9},{9,10},{10,11},{12,13},{... | collective-permute-start | bytes 786440 | tf_op jit(solution)/shard_map/ppermute | solution.py:21
  108.2 9.5 %collective-permute-start.11 = (f32[2,256,128]{2,1,0:T(8,128)S(1)}, f32[2,256,128]{2,1,0:T(8,128)S(1)}, u32[]{:S(2)}, u32[]{:S(2)}) collective-permute-start(f32[2,256,128]{2,1,0:T(8,128)S(1)} %get-tuple-element.34), channel_id=1, source_target_pairs={{1,0},{2,1},{3,2},{5,4},{6,5},{7,6},{9,8},{10,9},{11,10},{13,12},{... | collective-permute-start | bytes 786440 | tf_op jit(solution)/shard_map/ppermute | solution.py:21
  109.6 8.7 %collective-permute-start.12 = (f32[256,256]{1,0:T(8,128)S(1)}, f32[256,256]{1,0:T(8,128)S(1)}, u32[]{:S(2)}, u32[]{:S(2)}) collective-permute-start(f32[256,256]{1,0:T(8,128)S(1)} %get-tuple-element.28), channel_id=1, source_target_pairs={{0,4},{4,8},{8,12},{12,16},{16,20},{20,24},{24,28},{28,32},{32,36}... | collective-permute-start | bytes 786440 | tf_op jit(solution)/shard_map/ppermute | solution.py:21
  120.2 7.7 %collective-permute-start.14 = (f32[256,256]{1,0:T(8,128)S(1)}, f32[256,256]{1,0:T(8,128)S(1)}, u32[]{:S(2)}, u32[]{:S(2)}) collective-permute-start(f32[256,256]{1,0:T(8,128)S(1)} %get-tuple-element.25), channel_id=1, source_target_pairs={{4,0},{8,4},{12,8},{16,12},{20,16},{24,20},{28,24},{32,28},{36,32}... | collective-permute-start | bytes 786440 | tf_op jit(solution)/shard_map/ppermute | solution.py:21
  123.7 10.9 %collective-permute-start.15 = (f32[2,256,128]{2,1,0:T(8,128)S(1)}, f32[2,256,128]{2,1,0:T(8,128)S(1)}, u32[]{:S(2)}, u32[]{:S(2)}) collective-permute-start(f32[2,256,128]{2,1,0:T(8,128)S(1)} %slice.266), channel_id=1, source_target_pairs={{1,0},{2,1},{3,2},{5,4},{6,5},{7,6},{9,8},{10,9},{11,10},{13,12},{... | collective-permute-start | bytes 786440 | tf_op jit(solution)/shard_map/ppermute | solution.py:21
  125.1 9.6 %copy-start.1 = (f32[2,1,256,384]{3,2,1,0:T(8,128)S(1)}, f32[2,1,256,384]{3,2,1,0:T(8,128)}, u32[]{:S(2)}) copy-start(f32[2,1,256,384]{3,2,1,0:T(8,128)} %param.8) | copy-start | bytes 2359300

commit v4 on v3

--- a/solution.py
+++ b/solution.py
@@ -22,6 +22,7 @@
 
 
 def _pack_kernel(code_ref, tiles_ref, out_ref, *, per_owner, owner_subs, block_len):
+    out_ref[...] = jnp.zeros_like(out_ref)
     previous = jnp.int32(-1)
     rank = jnp.int32(0)
     for j in range(tiles_ref.shape[0]):

time: 137 us -> 137 us (level)
  no operation moved by 1% of the time
where the time goes in v4:
time: 137 us
  starting transfers between devices  53.1 us (39%)
  waiting for transfers between devices  36 us (26%)
  matrix products  17.2 us (13%)
  local copies, waits for them, and re-layouts  11.4 us (8%)
  other arithmetic  10.9 us (8%)
  Pallas kernels  6.63 us (5%)
    ppermute x16, starting transfers between devices, from_behind(): lax.ppermute(value, axis, [(source, source + steps) for source in range(i...  45.3 us
    ppermute x16, waiting for transfers between devices, from_behind(): lax.ppermute(value, axis, [(source, source + steps) for source in range(i...  36 us
    dot_general x1, matrix products, shards(): jnp.einsum('jka,jkb->jab', factor_panels[:, 0, 0], factor_panels[:, 0, 1]...  9.51 us
    all_to_all x1, starting transfers between devices, shards(): lax.all_to_all(send_tiles, 'gx', split_axis=0, concat_axis=0, tiled=True)  7.85 us
    dot_general x4, matrix products, shards(): jnp.einsum('ncm,nmk->nck', jnp.concatenate([high, low], axis=1), matrices...  7.7 us
    pallas_call x1, Pallas kernels, matrix_tiles(): pl.pallas_call(partial(_matrix_kernel, subs=subs, blocks=blocks, block_le...  3.5 us
    pallas_call x1, Pallas kernels, pack_tiles(): pl.pallas_call(partial(_pack_kernel, per_owner=per_owner, owner_subs=owne...  3.14 us
    unnamed x14, local copies, waits for them, and re-layouts  2.8 us
  transfers between devices with their start and end apart: 17, of which 9 were waited for; matrix products, arithmetic and copies ran while one was open for 12% of the time, Pallas kernels for 0%

profile of v4, /device:TPU:17, one launch (start us, length us, event | category | flops | bytes accessed | tf_op | source)
XLA Modules:
  0.0 136.5 jit_solution(12368117777381749731)
XLA Ops:
  0.6 9.5 %fusion.25.tiles_ref = bf16[26,128,128]{2,1,0:T(8,128)(2,1)} fusion(bf16[26,1,2,1536,128]{4,3,2,1,0:T(8,128)(2,1)} %param.7), kind=kOutput, calls=%fused_computation.41 | convolution fusion | flops 1309048832 | bytes 21299200 | tf_op jit(solution)/shard_map/jka,jkb->jab/dot_general | solution.py:139
  10.1 3.1 %shard_map.68 = bf16[8192,128]{1,0:T(8,128)(2,1)} custom-call(s32[26]{0:T(128)} %bitcast.127, bf16[26,128,128]{2,1,0:T(8,128)(2,1)} %fusion.25.tiles_ref), custom_call_target="tpu_custom_call" | custom-call | bytes 2949120 | tf_op jit(solution)/shard_map/pallas_call | solution.py:44
  13.3 7.8 %all-to-all-start = ((bf16[32,256,128]{2,1,0:T(8,128)(2,1)}), bf16[32,256,128]{2,1,0:T(8,128)(2,1)S(1)}, u32[]{:S(2)}, u32[]{:S(2)}) async-start(bf16[32,256,128]{2,1,0:T(8,128)(2,1)} %bitcast.113), calls=%async_computation | async-start | bytes 4194304 | tf_op jit(solution)/shard_map/all_to_all | solution.py:149
  21.8 2.1 %broadcast_multiply_fusion = (f32[2,256,384]{2,1,0:T(8,128)}, f32[2,256,384]{2,1,0:T(8,128)S(1)}) fusion(f32[2,384]{1,0:T(2,128)S(1)} %pad_convert_fusion, f32[2,1,256,384]{3,2,1,0:T(8,128)} %param.8), kind=kLoop, calls=%fused_computation.66 | loop fusion | flops 393216 | bytes 2362368 | tf_op jit(solution)/shard_map/div | solution.py:174
  24.7 3.4 %collective-permute-start = (f32[256,256]{1,0:T(8,128)}, f32[256,256]{1,0:T(8,128)S(1)}, u32[]{:S(2)}, u32[]{:S(2)}) collective-permute-start(f32[256,256]{1,0:T(8,128)} %slice_bitcast_fusion.7), channel_id=1, source_target_pairs={{0,4},{4,8},{8,12},{12,16},{16,20},{20,24},{24,28},{28,32},{32,36}... | collective-permute-start | bytes 786440 | tf_op jit(solution)/shard_map/ppermute | solution.py:21
  28.8 3.5 %collective-permute-start.1 = (f32[2,256,128]{2,1,0:T(8,128)}, f32[2,256,128]{2,1,0:T(8,128)S(1)}, u32[]{:S(2)}, u32[]{:S(2)}) collective-permute-start(f32[2,256,128]{2,1,0:T(8,128)} %slice.225), channel_id=1, source_target_pairs={{0,1},{1,2},{2,3},{4,5},{5,6},{6,7},{8,9},{9,10},{10,11},{12,13},{... | collective-permute-start | bytes 786440 | tf_op jit(solution)/shard_map/ppermute | solution.py:21
  32.4 1.7 %slice.226 = f32[2,256,128]{2,1,0:T(8,128)} slice(f32[2,256,384]{2,1,0:T(8,128)} %get-tuple-element.14), slice={[0:2], [0:256], [256:384]} | slice | bytes 524288 | tf_op jit(solution)/shard_map/slice | solution.py:181
  34.1 1.7 %slice.223 = f32[1,256,256]{2,1,0:T(8,128)} slice(f32[2,256,384]{2,1,0:T(8,128)} %get-tuple-element.14), slice={[0:1], [0:256], [0:256]} | slice | bytes 524288 | tf_op jit(solution)/shard_map/slice | solution.py:182
  35.8 1.9 %slice.224 = f32[2,256,256]{2,1,0:T(8,128)} slice(f32[2,256,384]{2,1,0:T(8,128)} %get-tuple-element.14), slice={[0:2], [0:256], [0:256]} | slice | bytes 1048576 | tf_op jit(solution)/shard_map/slice | solution.py:180
  39.7 8.3 %collective-permute-done = f32[256,256]{1,0:T(8,128)S(1)} collective-permute-done((f32[256,256]{1,0:T(8,128)}, f32[256,256]{1,0:T(8,128)S(1)}, u32[]{:S(2)}, u32[]{:S(2)}) %collective-permute-start) | collective-permute-done | bytes 262176 | tf_op jit(solution)/shard_map/ppermute | solution.py:21
  51.9 3.5 %shard_map.69 = bf16[2,768,768]{2,1,0:T(8,128)(2,1)} custom-call(s32[2,72]{1,0:T(2,128)} %pad_add_fusion.table_ref, bf16[64,128,128]{2,1,0:T(8,128)(2,1)} %bitcast.112), custom_call_target="tpu_custom_call" | custom-call | bytes 4456448 | tf_op jit(solution)/shard_map/pallas_call | solution.py:77
  55.4 3.5 %fusion.9 = f32[2,512,768]{2,1,0:T(8,128)S(1)} fusion(bf16[2,768,768]{2,1,0:T(8,128)(2,1)} %shard_map.69, bf16[2,256,768]{2,1,0:T(8,128)(2,1)} %get-tuple-element.52, bf16[2,256,768]{2,1,0:T(8,128)(2,1)} %get-tuple-element.51), kind=kOutput, calls=%fused_computation.22 | convolution fusion | flops 1211105280 | bytes 7077888 | tf_op jit(solution)/shard_map/ncm,nmk->nck/dot_general | solution.py:187
  59.2 4.4 %collective-permute-start.2 = (f32[256,256]{1,0:T(8,128)S(1)}, f32[256,256]{1,0:T(8,128)S(1)}, u32[]{:S(2)}, u32[]{:S(2)}) collective-permute-start(f32[256,256]{1,0:T(8,128)S(1)} %get-tuple-element.46), channel_id=1, source_target_pairs={{4,0},{8,4},{12,8},{16,12},{20,16},{24,20},{28,24},{32,28},{36,32}... | collective-permute-start | bytes 786440 | tf_op jit(solution)/shard_map/ppermute | solution.py:21
  63.6 3.6 %collective-permute-start.5 = (f32[2,256,128]{2,1,0:T(8,128)S(1)}, f32[2,256,128]{2,1,0:T(8,128)S(1)}, u32[]{:S(2)}, u32[]{:S(2)}) collective-permute-start(f32[2,256,128]{2,1,0:T(8,128)S(1)} %get-tuple-element.49), channel_id=1, source_target_pairs={{0,1},{1,2},{2,3},{4,5},{5,6},{6,7},{8,9},{9,10},{10,11},{12,13},{... | collective-permute-start | bytes 786440 | tf_op jit(solution)/shard_map/ppermute | solution.py:21
  68.5 2.1 %collective-permute-start.4 = (f32[256,256]{1,0:T(8,128)S(1)}, f32[256,256]{1,0:T(8,128)S(1)}, u32[]{:S(2)}, u32[]{:S(2)}) collective-permute-start(f32[256,256]{1,0:T(8,128)S(1)} %get-tuple-element.45), channel_id=1, source_target_pairs={{0,4},{4,8},{8,12},{12,16},{16,20},{20,24},{24,28},{28,32},{32,36}... | collective-permute-start | bytes 786440 | tf_op jit(solution)/shard_map/ppermute | solution.py:21
  70.7 2.1 %collective-permute-done.5 = f32[2,256,128]{2,1,0:T(8,128)S(1)} collective-permute-done((f32[2,256,128]{2,1,0:T(8,128)S(1)}, f32[2,256,128]{2,1,0:T(8,128)S(1)}, u32[]{:S(2)}, u32[]{:S(2)}) %collective-permute-start.5) | collective-permute-done | bytes 262176 | tf_op jit(solution)/shard_map/ppermute | solution.py:21
  72.8 4.2 %collective-permute-done.3 = f32[2,256,128]{2,1,0:T(8,128)S(1)} collective-permute-done((f32[2,256,128]{2,1,0:T(8,128)S(1)}, f32[2,256,128]{2,1,0:T(8,128)S(1)}, u32[]{:S(2)}, u32[]{:S(2)}) %collective-permute-start.3) | collective-permute-done | bytes 262176 | tf_op jit(solution)/shard_map/ppermute | solution.py:21
  77.7 1.4 %copy-done.2 = bf16[2,768,768]{2,1,0:T(8,128)(2,1)S(1)} copy-done((bf16[2,768,768]{2,1,0:T(8,128)(2,1)S(1)}, bf16[2,768,768]{2,1,0:T(8,128)(2,1)}, u32[]{:S(2)}) %copy-start.2) | copy-done | bytes 2359320
  80.8 3.1 %collective-permute-start.6 = (f32[256,256]{1,0:T(8,128)S(1)}, f32[256,256]{1,0:T(8,128)S(1)}, u32[]{:S(2)}, u32[]{:S(2)}) collective-permute-start(f32[256,256]{1,0:T(8,128)S(1)} %get-tuple-element.38), channel_id=1, source_target_pairs={{4,0},{8,4},{12,8},{16,12},{20,16},{24,20},{28,24},{32,28},{36,32}... | collective-permute-start | bytes 786440 | tf_op jit(solution)/shard_map/ppermute | solution.py:21
  84.0 4.3 %collective-permute-start.9 = (f32[2,256,128]{2,1,0:T(8,128)S(1)}, f32[2,256,128]{2,1,0:T(8,128)S(1)}, u32[]{:S(2)}, u32[]{:S(2)}) collective-permute-start(f32[2,256,128]{2,1,0:T(8,128)S(1)} %get-tuple-element.41), channel_id=1, source_target_pairs={{0,1},{1,2},{2,3},{4,5},{5,6},{6,7},{8,9},{9,10},{10,11},{12,13},{... | collective-permute-start | bytes 786440 | tf_op jit(solution)/shard_map/ppermute | solution.py:21
  89.5 1.9 %collective-permute-start.8 = (f32[256,256]{1,0:T(8,128)S(1)}, f32[256,256]{1,0:T(8,128)S(1)}, u32[]{:S(2)}, u32[]{:S(2)}) collective-permute-start(f32[256,256]{1,0:T(8,128)S(1)} %get-tuple-element.37), channel_id=1, source_target_pairs={{0,4},{4,8},{8,12},{12,16},{16,20},{20,24},{24,28},{28,32},{32,36}... | collective-permute-start | bytes 786440 | tf_op jit(solution)/shard_map/ppermute | solution.py:21
  91.6 1.8 %collective-permute-done.9 = f32[2,256,128]{2,1,0:T(8,128)S(1)} collective-permute-done((f32[2,256,128]{2,1,0:T(8,128)S(1)}, f32[2,256,128]{2,1,0:T(8,128)S(1)}, u32[]{:S(2)}, u32[]{:S(2)}) %collective-permute-start.9) | collective-permute-done | bytes 262176 | tf_op jit(solution)/shard_map/ppermute | solution.py:21
  93.3 4.2 %collective-permute-done.7 = f32[2,256,128]{2,1,0:T(8,128)S(1)} collective-permute-done((f32[2,256,128]{2,1,0:T(8,128)S(1)}, f32[2,256,128]{2,1,0:T(8,128)S(1)}, u32[]{:S(2)}, u32[]{:S(2)}) %collective-permute-start.7) | collective-permute-done | bytes 262176 | tf_op jit(solution)/shard_map/ppermute | solution.py:21
  100.0 4.1 %collective-permute-start.10 = (f32[256,256]{1,0:T(8,128)S(1)}, f32[256,256]{1,0:T(8,128)S(1)}, u32[]{:S(2)}, u32[]{:S(2)}) collective-permute-start(f32[256,256]{1,0:T(8,128)S(1)} %get-tuple-element.29), channel_id=1, source_target_pairs={{4,0},{8,4},{12,8},{16,12},{20,16},{24,20},{28,24},{32,28},{36,32}... | collective-permute-start | bytes 786440 | tf_op jit(solution)/shard_map/ppermute | solution.py:21
  104.2 4.3 %collective-permute-start.13 = (f32[2,256,128]{2,1,0:T(8,128)S(1)}, f32[2,256,128]{2,1,0:T(8,128)S(1)}, u32[]{:S(2)}, u32[]{:S(2)}) collective-permute-start(f32[2,256,128]{2,1,0:T(8,128)S(1)} %get-tuple-element.33), channel_id=1, source_target_pairs={{0,1},{1,2},{2,3},{4,5},{5,6},{6,7},{8,9},{9,10},{10,11},{12,13},{... | collective-permute-start | bytes 786440 | tf_op jit(solution)/shard_map/ppermute | solution.py:21
  109.9 2.1 %collective-permute-start.12 = (f32[256,256]{1,0:T(8,128)S(1)}, f32[256,256]{1,0:T(8,128)S(1)}, u32[]{:S(2)}, u32[]{:S(2)}) collective-permute-start(f32[256,256]{1,0:T(8,128)S(1)} %get-tuple-element.28), channel_id=1, source_target_pairs={{0,4},{4,8},{8,12},{12,16},{16,20},{20,24},{24,28},{28,32},{32,36}... | collective-permute-start | bytes 786440 | tf_op jit(solution)/shard_map/ppermute | solution.py:21
  112.0 2.0 %collective-permute-done.13 = f32[2,256,128]{2,1,0:T(8,128)S(1)} collective-permute-done((f32[2,256,128]{2,1,0:T(8,128)S(1)}, f32[2,256,128]{2,1,0:T(8,128)S(1)}, u32[]{:S(2)}, u32[]{:S(2)}) %collective-permute-start.13) | collective-permute-done | bytes 262176 | tf_op jit(solution)/shard_map/ppermute | solution.py:21
  114.1 3.8 %collective-permute-done.11 = f32[2,256,128]{2,1,0:T(8,128)S(1)} collective-permute-done((f32[2,256,128]{2,1,0:T(8,128)S(1)}, f32[2,256,128]{2,1,0:T(8,128)S(1)}, u32[]{:S(2)}, u32[]{:S(2)}) %collective-permute-start.11) | collective-permute-done | bytes 262176 | tf_op jit(solution)/shard_map/ppermute | solution.py:21
  120.5 3.3 %collective-permute-start.14 = (f32[256,256]{1,0:T(8,128)S(1)}, f32[256,256]{1,0:T(8,128)S(1)}, u32[]{:S(2)}, u32[]{:S(2)}) collective-permute-start(f32[256,256]{1,0:T(8,128)S(1)} %get-tuple-element.25), channel_id=1, source_target_pairs={{4,0},{8,4},{12,8},{16,12},{20,16},{24,20},{28,24},{32,28},{36,32}... | collective-permute-start | bytes 786440 | tf_op jit(solution)/shard_map/ppermute | solution.py:21
  125.3 2.9 %collective-permute-done.14 = f32[256,256]{1,0:T(8,128)S(1)} collective-permute-done((f32[256,256]{1,0:T(8,128)S(1)}, f32[256,256]{1,0:T(8,128)S(1)}, u32[]{:S(2)}, u32[]{:S(2)}) %collective-permute-start.14) | collective-permute-done | bytes 262176 | tf_op jit(solution)/shard_map/ppermute | solution.py:21
  128.3 6.6 %collective-permute-done.15 = f32[2,256,128]{2,1,0:T(8,128)S(1)} collective-permute-done((f32[2,256,128]{2,1,0:T(8,128)S(1)}, f32[2,256,128]{2,1,0:T(8,128)S(1)}, u32[]{:S(2)}, u32[]{:S(2)}) %collective-permute-start.15) | collective-permute-done | bytes 262176 | tf_op jit(solution)/shard_map/ppermute | solution.py:21
  134.9 1.6 %fusion.32 = (f32[2,1,256,384]{3,2,1,0:T(8,128)}, f32[2,1,256,384]{3,2,1,0:T(8,128)}) fusion(f32[2,1,256,128]{3,2,0,1:T(8,128)S(1)} %fusion.34, f32[2,1,256,256]{3,2,0,1:T(8,128)S(1)} %fusion.33, f32[2,1,256,128]{3,2,0,1:T(8,128)S(1)} %bitcast.117, f32[2,1,256,256]{3,2,0,1:T(8,128)S(1)} %fusion.61, f32[2,1,256,128]{3,2,0,1:T(8,128)S(1)} %bitcast.116, ...), kind=kLoop, calls=%fused_computation.51 | loop fusion | flops 4325376 | bytes 5508096
  (113 shorter events, 21.2 us)
Async XLA Ops:
  13.3 7.9 %copy-start.5 = (s32[64,1]{0,1:T(1,128)S(1)}, s32[64,1]{0,1:T(1,128)}, u32[]{:S(2)}) copy-start(s32[64,1]{0,1:T(1,128)} %param.5) | copy-start | bytes 772
  13.3 37.2 %all-to-all-start = ((bf16[32,256,128]{2,1,0:T(8,128)(2,1)}), bf16[32,256,128]{2,1,0:T(8,128)(2,1)S(1)}, u32[]{:S(2)}, u32[]{:S(2)}) async-start(bf16[32,256,128]{2,1,0:T(8,128)(2,1)} %bitcast.113), calls=%async_computation | async-start | bytes 4194304 | tf_op jit(solution)/shard_map/all_to_all | solution.py:149
  24.0 14.2 %copy-start.6 = (s32[6]{0:T(128)S(1)}, s32[6]{0:T(128)}, u32[]{:S(2)}) copy-start(s32[6]{0:T(128)} %constant.128.clone) | copy-start | bytes 76
  24.7 23.4 %collective-permute-start = (f32[256,256]{1,0:T(8,128)}, f32[256,256]{1,0:T(8,128)S(1)}, u32[]{:S(2)}, u32[]{:S(2)}) collective-permute-start(f32[256,256]{1,0:T(8,128)} %slice_bitcast_fusion.7), channel_id=1, source_target_pairs={{0,4},{4,8},{8,12},{12,16},{16,20},{20,24},{24,28},{28,32},{32,36}... | collective-permute-start | bytes 786440 | tf_op jit(solution)/shard_map/ppermute | solution.py:21
  28.8 20.3 %collective-permute-start.1 = (f32[2,256,128]{2,1,0:T(8,128)}, f32[2,256,128]{2,1,0:T(8,128)S(1)}, u32[]{:S(2)}, u32[]{:S(2)}) collective-permute-start(f32[2,256,128]{2,1,0:T(8,128)} %slice.225), channel_id=1, source_target_pairs={{0,1},{1,2},{2,3},{4,5},{5,6},{6,7},{8,9},{9,10},{10,11},{12,13},{... | collective-permute-start | bytes 786440 | tf_op jit(solution)/shard_map/ppermute | solution.py:21
  39.0 10.1 %copy-start.3 = (f32[2,256,256]{2,1,0:T(8,128)S(1)}, f32[2,256,256]{2,1,0:T(8,128)}, u32[]{:S(2)}) copy-start(f32[2,256,256]{2,1,0:T(8,128)} %slice.224) | copy-start | bytes 1572868
  39.1 10.1 %copy-start.4 = (f32[2,256,128]{2,1,0:T(8,128)S(1)}, f32[2,256,128]{2,1,0:T(8,128)}, u32[]{:S(2)}) copy-start(f32[2,256,128]{2,1,0:T(8,128)} %slice.226) | copy-start | bytes 786436
  50.5 1.4 copy-start
  59.2 11.4 %collective-permute-start.2 = (f32[256,256]{1,0:T(8,128)S(1)}, f32[256,256]{1,0:T(8,128)S(1)}, u32[]{:S(2)}, u32[]{:S(2)}) collective-permute-start(f32[256,256]{1,0:T(8,128)S(1)} %get-tuple-element.46), channel_id=1, source_target_pairs={{4,0},{8,4},{12,8},{16,12},{20,16},{24,20},{28,24},{32,28},{36,32}... | collective-permute-start | bytes 786440 | tf_op jit(solution)/shard_map/ppermute | solution.py:21
  63.6 9.2 %collective-permute-start.5 = (f32[2,256,128]{2,1,0:T(8,128)S(1)}, f32[2,256,128]{2,1,0:T(8,128)S(1)}, u32[]{:S(2)}, u32[]{:S(2)}) collective-permute-start(f32[2,256,128]{2,1,0:T(8,128)S(1)} %get-tuple-element.49), channel_id=1, source_target_pairs={{0,1},{1,2},{2,3},{4,5},{5,6},{6,7},{8,9},{9,10},{10,11},{12,13},{... | collective-permute-start | bytes 786440 | tf_op jit(solution)/shard_map/ppermute | solution.py:21
  67.2 9.8 %collective-permute-start.3 = (f32[2,256,128]{2,1,0:T(8,128)S(1)}, f32[2,256,128]{2,1,0:T(8,128)S(1)}, u32[]{:S(2)}, u32[]{:S(2)}) collective-permute-start(f32[2,256,128]{2,1,0:T(8,128)S(1)} %get-tuple-element.50), channel_id=1, source_target_pairs={{1,0},{2,1},{3,2},{5,4},{6,5},{7,6},{9,8},{10,9},{11,10},{13,12},{... | collective-permute-start | bytes 786440 | tf_op jit(solution)/shard_map/ppermute | solution.py:21
  68.5 8.8 %collective-permute-start.4 = (f32[256,256]{1,0:T(8,128)S(1)}, f32[256,256]{1,0:T(8,128)S(1)}, u32[]{:S(2)}, u32[]{:S(2)}) collective-permute-start(f32[256,256]{1,0:T(8,128)S(1)} %get-tuple-element.45), channel_id=1, source_target_pairs={{0,4},{4,8},{8,12},{12,16},{16,20},{20,24},{24,28},{28,32},{32,36}... | collective-permute-start | bytes 786440 | tf_op jit(solution)/shard_map/ppermute | solution.py:21
  77.4 1.7 %copy-start.2 = (bf16[2,768,768]{2,1,0:T(8,128)(2,1)S(1)}, bf16[2,768,768]{2,1,0:T(8,128)(2,1)}, u32[]{:S(2)}) copy-start(bf16[2,768,768]{2,1,0:T(8,128)(2,1)} %shard_map.69) | copy-start | bytes 7077892
  80.8 10.7 %collective-permute-start.6 = (f32[256,256]{1,0:T(8,128)S(1)}, f32[256,256]{1,0:T(8,128)S(1)}, u32[]{:S(2)}, u32[]{:S(2)}) collective-permute-start(f32[256,256]{1,0:T(8,128)S(1)} %get-tuple-element.38), channel_id=1, source_target_pairs={{4,0},{8,4},{12,8},{16,12},{20,16},{24,20},{28,24},{32,28},{36,32}... | collective-permute-start | bytes 786440 | tf_op jit(solution)/shard_map/ppermute | solution.py:21
  84.0 9.4 %collective-permute-start.9 = (f32[2,256,128]{2,1,0:T(8,128)S(1)}, f32[2,256,128]{2,1,0:T(8,128)S(1)}, u32[]{:S(2)}, u32[]{:S(2)}) collective-permute-start(f32[2,256,128]{2,1,0:T(8,128)S(1)} %get-tuple-element.41), channel_id=1, source_target_pairs={{0,1},{1,2},{2,3},{4,5},{5,6},{6,7},{8,9},{9,10},{10,11},{12,13},{... | collective-permute-start | bytes 786440 | tf_op jit(solution)/shard_map/ppermute | solution.py:21
  88.2 9.2 %collective-permute-start.7 = (f32[2,256,128]{2,1,0:T(8,128)S(1)}, f32[2,256,128]{2,1,0:T(8,128)S(1)}, u32[]{:S(2)}, u32[]{:S(2)}) collective-permute-start(f32[2,256,128]{2,1,0:T(8,128)S(1)} %get-tuple-element.42), channel_id=1, source_target_pairs={{1,0},{2,1},{3,2},{5,4},{6,5},{7,6},{9,8},{10,9},{11,10},{13,12},{... | collective-permute-start | bytes 786440 | tf_op jit(solution)/shard_map/ppermute | solution.py:21
  89.5 8.4 %collective-permute-start.8 = (f32[256,256]{1,0:T(8,128)S(1)}, f32[256,256]{1,0:T(8,128)S(1)}, u32[]{:S(2)}, u32[]{:S(2)}) collective-permute-start(f32[256,256]{1,0:T(8,128)S(1)} %get-tuple-element.37), channel_id=1, source_target_pairs={{0,4},{4,8},{8,12},{12,16},{16,20},{20,24},{24,28},{28,32},{32,36}... | collective-permute-start | bytes 786440 | tf_op jit(solution)/shard_map/ppermute | solution.py:21
  100.0 12.0 %collective-permute-start.10 = (f32[256,256]{1,0:T(8,128)S(1)}, f32[256,256]{1,0:T(8,128)S(1)}, u32[]{:S(2)}, u32[]{:S(2)}) collective-permute-start(f32[256,256]{1,0:T(8,128)S(1)} %get-tuple-element.29), channel_id=1, source_target_pairs={{4,0},{8,4},{12,8},{16,12},{20,16},{24,20},{28,24},{32,28},{36,32}... | collective-permute-start | bytes 786440 | tf_op jit(solution)/shard_map/ppermute | solution.py:21
  104.2 9.9 %collective-permute-start.13 = (f32[2,256,128]{2,1,0:T(8,128)S(1)}, f32[2,256,128]{2,1,0:T(8,128)S(1)}, u32[]{:S(2)}, u32[]{:S(2)}) collective-permute-start(f32[2,256,128]{2,1,0:T(8,128)S(1)} %get-tuple-element.33), channel_id=1, source_target_pairs={{0,1},{1,2},{2,3},{4,5},{5,6},{6,7},{8,9},{9,10},{10,11},{12,13},{... | collective-permute-start | bytes 786440 | tf_op jit(solution)/shard_map/ppermute | solution.py:21
  108.5 9.5 %collective-permute-start.11 = (f32[2,256,128]{2,1,0:T(8,128)S(1)}, f32[2,256,128]{2,1,0:T(8,128)S(1)}, u32[]{:S(2)}, u32[]{:S(2)}) collective-permute-start(f32[2,256,128]{2,1,0:T(8,128)S(1)} %get-tuple-element.34), channel_id=1, source_target_pairs={{1,0},{2,1},{3,2},{5,4},{6,5},{7,6},{9,8},{10,9},{11,10},{13,12},{... | collective-permute-start | bytes 786440 | tf_op jit(solution)/shard_map/ppermute | solution.py:21
  109.9 8.7 %collective-permute-start.12 = (f32[256,256]{1,0:T(8,128)S(1)}, f32[256,256]{1,0:T(8,128)S(1)}, u32[]{:S(2)}, u32[]{:S(2)}) collective-permute-start(f32[256,256]{1,0:T(8,128)S(1)} %get-tuple-element.28), channel_id=1, source_target_pairs={{0,4},{4,8},{8,12},{12,16},{16,20},{20,24},{24,28},{28,32},{32,36}... | collective-permute-start | bytes 786440 | tf_op jit(solution)/shard_map/ppermute | solution.py:21
  120.5 7.7 %collective-permute-start.14 = (f32[256,256]{1,0:T(8,128)S(1)}, f32[256,256]{1,0:T(8,128)S(1)}, u32[]{:S(2)}, u32[]{:S(2)}) collective-permute-start(f32[256,256]{1,0:T(8,128)S(1)} %get-tuple-element.25), channel_id=1, source_target_pairs={{4,0},{8,4},{12,8},{16,12},{20,16},{24,20},{28,24},{32,28},{36,32}... | collective-permute-start | bytes 786440 | tf_op jit(solution)/shard_map/ppermute | solution.py:21
  124.0 10.9 %collective-permute-start.15 = (f32[2,256,128]{2,1,0:T(8,128)S(1)}, f32[2,256,128]{2,1,0:T(8,128)S(1)}, u32[]{:S(2)}, u32[]{:S(2)}) collective-permute-start(f32[2,256,128]{2,1,0:T(8,128)S(1)} %slice.266), channel_id=1, source_target_pairs={{1,0},{2,1},{3,2},{5,4},{6,5},{7,6},{9,8},{10,9},{11,10},{13,12},{... | collective-permute-start | bytes 786440 | tf_op jit(solution)/shard_map/ppermute | solution.py:21
  125.3 9.6 %copy-start.1 = (f32[2,1,256,384]{3,2,1,0:T(8,128)S(1)}, f32[2,1,256,384]{3,2,1,0:T(8,128)}, u32[]{:S(2)}) copy-start(f32[2,1,256,384]{3,2,1,0:T(8,128)} %param.8) | copy-start | bytes 2359300

commit v5 on v2

--- a/solution.py
+++ b/solution.py
@@ -22,7 +22,6 @@
 
 
 def _pack_kernel(code_ref, tiles_ref, out_ref, *, per_owner, owner_subs, block_len):
-    out_ref[...] = jnp.zeros_like(out_ref)
     previous = jnp.int32(-1)
     rank = jnp.int32(0)
     for j in range(tiles_ref.shape[0]):

time: 137 us -> 137 us (level)
  no operation moved by 1% of the time
where the time goes in v5:
time: 137 us; the launch traced here: 136 us
  starting transfers between devices  53.1 us (39%)
  waiting for transfers between devices  36 us (26%)
  matrix products  17.2 us (13%)
  local copies, waits for them, and re-layouts  11.4 us (8%)
  other arithmetic  10.9 us (8%)
  Pallas kernels  6.34 us (5%)
    ppermute x16, starting transfers between devices, from_behind(): lax.ppermute(value, axis, [(source, source + steps) for source in range(i...  45.3 us
    ppermute x16, waiting for transfers between devices, from_behind(): lax.ppermute(value, axis, [(source, source + steps) for source in range(i...  36 us
    dot_general x1, matrix products, shards(): jnp.einsum('jka,jkb->jab', factor_panels[:, 0, 0], factor_panels[:, 0, 1]...  9.51 us
    all_to_all x1, starting transfers between devices, shards(): lax.all_to_all(send_tiles, 'gx', split_axis=0, concat_axis=0, tiled=True)  7.85 us
    dot_general x4, matrix products, shards(): jnp.einsum('ncm,nmk->nck', jnp.concatenate([high, low], axis=1), matrices...  7.7 us
    pallas_call x1, Pallas kernels, matrix_tiles(): pl.pallas_call(partial(_matrix_kernel, subs=subs, blocks=blocks, block_le...  3.46 us
    pallas_call x1, Pallas kernels, pack_tiles(): pl.pallas_call(partial(_pack_kernel, per_owner=per_owner, owner_subs=owne...  2.88 us
    unnamed x14, local copies, waits for them, and re-layouts  2.8 us
  transfers between devices with their start and end apart: 17, of which 9 were waited for; matrix products, arithmetic and copies ran while one was open for 12% of the time, Pallas kernels for 0%

profile of v5, /device:TPU:17, one launch (start us, length us, event | category | flops | bytes accessed | tf_op | source)
XLA Modules:
  0.0 136.3 jit_solution(15190543241634624618)
XLA Ops:
  0.6 9.5 %fusion.25.tiles_ref = bf16[26,128,128]{2,1,0:T(8,128)(2,1)} fusion(bf16[26,1,2,1536,128]{4,3,2,1,0:T(8,128)(2,1)} %param.7), kind=kOutput, calls=%fused_computation.41 | convolution fusion | flops 1309048832 | bytes 21299200 | tf_op jit(solution)/shard_map/jka,jkb->jab/dot_general | solution.py:138
  10.1 2.9 %shard_map.68 = bf16[8192,128]{1,0:T(8,128)(2,1)} custom-call(s32[26]{0:T(128)} %bitcast.127, bf16[26,128,128]{2,1,0:T(8,128)(2,1)} %fusion.25.tiles_ref), custom_call_target="tpu_custom_call" | custom-call | bytes 2949120 | tf_op jit(solution)/shard_map/pallas_call | solution.py:43
  13.0 7.8 %all-to-all-start = ((bf16[32,256,128]{2,1,0:T(8,128)(2,1)}), bf16[32,256,128]{2,1,0:T(8,128)(2,1)S(1)}, u32[]{:S(2)}, u32[]{:S(2)}) async-start(bf16[32,256,128]{2,1,0:T(8,128)(2,1)} %bitcast.113), calls=%async_computation | async-start | bytes 4194304 | tf_op jit(solution)/shard_map/all_to_all | solution.py:148
  21.6 2.1 %broadcast_multiply_fusion = (f32[2,256,384]{2,1,0:T(8,128)}, f32[2,256,384]{2,1,0:T(8,128)S(1)}) fusion(f32[2,384]{1,0:T(2,128)S(1)} %pad_convert_fusion, f32[2,1,256,384]{3,2,1,0:T(8,128)} %param.8), kind=kLoop, calls=%fused_computation.66 | loop fusion | flops 393216 | bytes 2362368 | tf_op jit(solution)/shard_map/div | solution.py:173
  24.4 3.4 %collective-permute-start = (f32[256,256]{1,0:T(8,128)}, f32[256,256]{1,0:T(8,128)S(1)}, u32[]{:S(2)}, u32[]{:S(2)}) collective-permute-start(f32[256,256]{1,0:T(8,128)} %slice_bitcast_fusion.7), channel_id=1, source_target_pairs={{0,4},{4,8},{8,12},{12,16},{16,20},{20,24},{24,28},{28,32},{32,36}... | collective-permute-start | bytes 786440 | tf_op jit(solution)/shard_map/ppermute | solution.py:21
  28.5 3.5 %collective-permute-start.1 = (f32[2,256,128]{2,1,0:T(8,128)}, f32[2,256,128]{2,1,0:T(8,128)S(1)}, u32[]{:S(2)}, u32[]{:S(2)}) collective-permute-start(f32[2,256,128]{2,1,0:T(8,128)} %slice.225), channel_id=1, source_target_pairs={{0,1},{1,2},{2,3},{4,5},{5,6},{6,7},{8,9},{9,10},{10,11},{12,13},{... | collective-permute-start | bytes 786440 | tf_op jit(solution)/shard_map/ppermute | solution.py:21
  32.2 1.7 %slice.226 = f32[2,256,128]{2,1,0:T(8,128)} slice(f32[2,256,384]{2,1,0:T(8,128)} %get-tuple-element.14), slice={[0:2], [0:256], [256:384]} | slice | bytes 524288 | tf_op jit(solution)/shard_map/slice | solution.py:180
  33.8 1.7 %slice.223 = f32[1,256,256]{2,1,0:T(8,128)} slice(f32[2,256,384]{2,1,0:T(8,128)} %get-tuple-element.14), slice={[0:1], [0:256], [0:256]} | slice | bytes 524288 | tf_op jit(solution)/shard_map/slice | solution.py:181
  35.5 1.9 %slice.224 = f32[2,256,256]{2,1,0:T(8,128)} slice(f32[2,256,384]{2,1,0:T(8,128)} %get-tuple-element.14), slice={[0:2], [0:256], [0:256]} | slice | bytes 1048576 | tf_op jit(solution)/shard_map/slice | solution.py:179
  39.5 8.3 %collective-permute-done = f32[256,256]{1,0:T(8,128)S(1)} collective-permute-done((f32[256,256]{1,0:T(8,128)}, f32[256,256]{1,0:T(8,128)S(1)}, u32[]{:S(2)}, u32[]{:S(2)}) %collective-permute-start) | collective-permute-done | bytes 262176 | tf_op jit(solution)/shard_map/ppermute | solution.py:21
  51.6 3.5 %shard_map.69 = bf16[2,768,768]{2,1,0:T(8,128)(2,1)} custom-call(s32[2,72]{1,0:T(2,128)} %pad_add_fusion.table_ref, bf16[64,128,128]{2,1,0:T(8,128)(2,1)} %bitcast.112), custom_call_target="tpu_custom_call" | custom-call | bytes 4456448 | tf_op jit(solution)/shard_map/pallas_call | solution.py:76
  55.1 3.5 %fusion.9 = f32[2,512,768]{2,1,0:T(8,128)S(1)} fusion(bf16[2,768,768]{2,1,0:T(8,128)(2,1)} %shard_map.69, bf16[2,256,768]{2,1,0:T(8,128)(2,1)} %get-tuple-element.52, bf16[2,256,768]{2,1,0:T(8,128)(2,1)} %get-tuple-element.51), kind=kOutput, calls=%fused_computation.22 | convolution fusion | flops 1211105280 | bytes 7077888 | tf_op jit(solution)/shard_map/ncm,nmk->nck/dot_general | solution.py:186
  58.9 4.4 %collective-permute-start.2 = (f32[256,256]{1,0:T(8,128)S(1)}, f32[256,256]{1,0:T(8,128)S(1)}, u32[]{:S(2)}, u32[]{:S(2)}) collective-permute-start(f32[256,256]{1,0:T(8,128)S(1)} %get-tuple-element.46), channel_id=1, source_target_pairs={{4,0},{8,4},{12,8},{16,12},{20,16},{24,20},{28,24},{32,28},{36,32}... | collective-permute-start | bytes 786440 | tf_op jit(solution)/shard_map/ppermute | solution.py:21
  63.3 3.6 %collective-permute-start.5 = (f32[2,256,128]{2,1,0:T(8,128)S(1)}, f32[2,256,128]{2,1,0:T(8,128)S(1)}, u32[]{:S(2)}, u32[]{:S(2)}) collective-permute-start(f32[2,256,128]{2,1,0:T(8,128)S(1)} %get-tuple-element.49), channel_id=1, source_target_pairs={{0,1},{1,2},{2,3},{4,5},{5,6},{6,7},{8,9},{9,10},{10,11},{12,13},{... | collective-permute-start | bytes 786440 | tf_op jit(solution)/shard_map/ppermute | solution.py:21
  68.2 2.1 %collective-permute-start.4 = (f32[256,256]{1,0:T(8,128)S(1)}, f32[256,256]{1,0:T(8,128)S(1)}, u32[]{:S(2)}, u32[]{:S(2)}) collective-permute-start(f32[256,256]{1,0:T(8,128)S(1)} %get-tuple-element.45), channel_id=1, source_target_pairs={{0,4},{4,8},{8,12},{12,16},{16,20},{20,24},{24,28},{28,32},{32,36}... | collective-permute-start | bytes 786440 | tf_op jit(solution)/shard_map/ppermute | solution.py:21
  70.4 2.1 %collective-permute-done.5 = f32[2,256,128]{2,1,0:T(8,128)S(1)} collective-permute-done((f32[2,256,128]{2,1,0:T(8,128)S(1)}, f32[2,256,128]{2,1,0:T(8,128)S(1)}, u32[]{:S(2)}, u32[]{:S(2)}) %collective-permute-start.5) | collective-permute-done | bytes 262176 | tf_op jit(solution)/shard_map/ppermute | solution.py:21
  72.5 4.2 %collective-permute-done.3 = f32[2,256,128]{2,1,0:T(8,128)S(1)} collective-permute-done((f32[2,256,128]{2,1,0:T(8,128)S(1)}, f32[2,256,128]{2,1,0:T(8,128)S(1)}, u32[]{:S(2)}, u32[]{:S(2)}) %collective-permute-start.3) | collective-permute-done | bytes 262176 | tf_op jit(solution)/shard_map/ppermute | solution.py:21
  77.4 1.4 %copy-done.2 = bf16[2,768,768]{2,1,0:T(8,128)(2,1)S(1)} copy-done((bf16[2,768,768]{2,1,0:T(8,128)(2,1)S(1)}, bf16[2,768,768]{2,1,0:T(8,128)(2,1)}, u32[]{:S(2)}) %copy-start.2) | copy-done | bytes 2359320
  80.5 3.1 %collective-permute-start.6 = (f32[256,256]{1,0:T(8,128)S(1)}, f32[256,256]{1,0:T(8,128)S(1)}, u32[]{:S(2)}, u32[]{:S(2)}) collective-permute-start(f32[256,256]{1,0:T(8,128)S(1)} %get-tuple-element.38), channel_id=1, source_target_pairs={{4,0},{8,4},{12,8},{16,12},{20,16},{24,20},{28,24},{32,28},{36,32}... | collective-permute-start | bytes 786440 | tf_op jit(solution)/shard_map/ppermute | solution.py:21
  83.7 4.3 %collective-permute-start.9 = (f32[2,256,128]{2,1,0:T(8,128)S(1)}, f32[2,256,128]{2,1,0:T(8,128)S(1)}, u32[]{:S(2)}, u32[]{:S(2)}) collective-permute-start(f32[2,256,128]{2,1,0:T(8,128)S(1)} %get-tuple-element.41), channel_id=1, source_target_pairs={{0,1},{1,2},{2,3},{4,5},{5,6},{6,7},{8,9},{9,10},{10,11},{12,13},{... | collective-permute-start | bytes 786440 | tf_op jit(solution)/shard_map/ppermute | solution.py:21
  89.2 1.9 %collective-permute-start.8 = (f32[256,256]{1,0:T(8,128)S(1)}, f32[256,256]{1,0:T(8,128)S(1)}, u32[]{:S(2)}, u32[]{:S(2)}) collective-permute-start(f32[256,256]{1,0:T(8,128)S(1)} %get-tuple-element.37), channel_id=1, source_target_pairs={{0,4},{4,8},{8,12},{12,16},{16,20},{20,24},{24,28},{28,32},{32,36}... | collective-permute-start | bytes 786440 | tf_op jit(solution)/shard_map/ppermute | solution.py:21
  91.3 1.8 %collective-permute-done.9 = f32[2,256,128]{2,1,0:T(8,128)S(1)} collective-permute-done((f32[2,256,128]{2,1,0:T(8,128)S(1)}, f32[2,256,128]{2,1,0:T(8,128)S(1)}, u32[]{:S(2)}, u32[]{:S(2)}) %collective-permute-start.9) | collective-permute-done | bytes 262176 | tf_op jit(solution)/shard_map/ppermute | solution.py:21
  93.0 4.2 %collective-permute-done.7 = f32[2,256,128]{2,1,0:T(8,128)S(1)} collective-permute-done((f32[2,256,128]{2,1,0:T(8,128)S(1)}, f32[2,256,128]{2,1,0:T(8,128)S(1)}, u32[]{:S(2)}, u32[]{:S(2)}) %collective-permute-start.7) | collective-permute-done | bytes 262176 | tf_op jit(solution)/shard_map/ppermute | solution.py:21
  99.7 4.1 %collective-permute-start.10 = (f32[256,256]{1,0:T(8,128)S(1)}, f32[256,256]{1,0:T(8,128)S(1)}, u32[]{:S(2)}, u32[]{:S(2)}) collective-permute-start(f32[256,256]{1,0:T(8,128)S(1)} %get-tuple-element.29), channel_id=1, source_target_pairs={{4,0},{8,4},{12,8},{16,12},{20,16},{24,20},{28,24},{32,28},{36,32}... | collective-permute-start | bytes 786440 | tf_op jit(solution)/shard_map/ppermute | solution.py:21
  103.9 4.3 %collective-permute-start.13 = (f32[2,256,128]{2,1,0:T(8,128)S(1)}, f32[2,256,128]{2,1,0:T(8,128)S(1)}, u32[]{:S(2)}, u32[]{:S(2)}) collective-permute-start(f32[2,256,128]{2,1,0:T(8,128)S(1)} %get-tuple-element.33), channel_id=1, source_target_pairs={{0,1},{1,2},{2,3},{4,5},{5,6},{6,7},{8,9},{9,10},{10,11},{12,13},{... | collective-permute-start | bytes 786440 | tf_op jit(solution)/shard_map/ppermute | solution.py:21
  109.6 2.1 %collective-permute-start.12 = (f32[256,256]{1,0:T(8,128)S(1)}, f32[256,256]{1,0:T(8,128)S(1)}, u32[]{:S(2)}, u32[]{:S(2)}) collective-permute-start(f32[256,256]{1,0:T(8,128)S(1)} %get-tuple-element.28), channel_id=1, source_target_pairs={{0,4},{4,8},{8,12},{12,16},{16,20},{20,24},{24,28},{28,32},{32,36}... | collective-permute-start | bytes 786440 | tf_op jit(solution)/shard_map/ppermute | solution.py:21
  111.8 2.0 %collective-permute-done.13 = f32[2,256,128]{2,1,0:T(8,128)S(1)} collective-permute-done((f32[2,256,128]{2,1,0:T(8,128)S(1)}, f32[2,256,128]{2,1,0:T(8,128)S(1)}, u32[]{:S(2)}, u32[]{:S(2)}) %collective-permute-start.13) | collective-permute-done | bytes 262176 | tf_op jit(solution)/shard_map/ppermute | solution.py:21
  113.8 3.8 %collective-permute-done.11 = f32[2,256,128]{2,1,0:T(8,128)S(1)} collective-permute-done((f32[2,256,128]{2,1,0:T(8,128)S(1)}, f32[2,256,128]{2,1,0:T(8,128)S(1)}, u32[]{:S(2)}, u32[]{:S(2)}) %collective-permute-start.11) | collective-permute-done | bytes 262176 | tf_op jit(solution)/shard_map/ppermute | solution.py:21
  120.2 3.3 %collective-permute-start.14 = (f32[256,256]{1,0:T(8,128)S(1)}, f32[256,256]{1,0:T(8,128)S(1)}, u32[]{:S(2)}, u32[]{:S(2)}) collective-permute-start(f32[256,256]{1,0:T(8,128)S(1)} %get-tuple-element.25), channel_id=1, source_target_pairs={{4,0},{8,4},{12,8},{16,12},{20,16},{24,20},{28,24},{32,28},{36,32}... | collective-permute-start | bytes 786440 | tf_op jit(solution)/shard_map/ppermute | solution.py:21
  125.0 2.9 %collective-permute-done.14 = f32[256,256]{1,0:T(8,128)S(1)} collective-permute-done((f32[256,256]{1,0:T(8,128)S(1)}, f32[256,256]{1,0:T(8,128)S(1)}, u32[]{:S(2)}, u32[]{:S(2)}) %collective-permute-start.14) | collective-permute-done | bytes 262176 | tf_op jit(solution)/shard_map/ppermute | solution.py:21
  128.0 6.6 %collective-permute-done.15 = f32[2,256,128]{2,1,0:T(8,128)S(1)} collective-permute-done((f32[2,256,128]{2,1,0:T(8,128)S(1)}, f32[2,256,128]{2,1,0:T(8,128)S(1)}, u32[]{:S(2)}, u32[]{:S(2)}) %collective-permute-start.15) | collective-permute-done | bytes 262176 | tf_op jit(solution)/shard_map/ppermute | solution.py:21
  134.6 1.6 %fusion.32 = (f32[2,1,256,384]{3,2,1,0:T(8,128)}, f32[2,1,256,384]{3,2,1,0:T(8,128)}) fusion(f32[2,1,256,128]{3,2,0,1:T(8,128)S(1)} %fusion.34, f32[2,1,256,256]{3,2,0,1:T(8,128)S(1)} %fusion.33, f32[2,1,256,128]{3,2,0,1:T(8,128)S(1)} %bitcast.117, f32[2,1,256,256]{3,2,0,1:T(8,128)S(1)} %fusion.61, f32[2,1,256,128]{3,2,0,1:T(8,128)S(1)} %bitcast.116, ...), kind=kLoop, calls=%fused_computation.51 | loop fusion | flops 4325376 | bytes 5508096
  (113 shorter events, 21.2 us)
Async XLA Ops:
  13.0 7.9 %copy-start.5 = (s32[64,1]{0,1:T(1,128)S(1)}, s32[64,1]{0,1:T(1,128)}, u32[]{:S(2)}) copy-start(s32[64,1]{0,1:T(1,128)} %param.5) | copy-start | bytes 772
  13.0 37.2 %all-to-all-start = ((bf16[32,256,128]{2,1,0:T(8,128)(2,1)}), bf16[32,256,128]{2,1,0:T(8,128)(2,1)S(1)}, u32[]{:S(2)}, u32[]{:S(2)}) async-start(bf16[32,256,128]{2,1,0:T(8,128)(2,1)} %bitcast.113), calls=%async_computation | async-start | bytes 4194304 | tf_op jit(solution)/shard_map/all_to_all | solution.py:148
  23.7 14.2 %copy-start.6 = (s32[6]{0:T(128)S(1)}, s32[6]{0:T(128)}, u32[]{:S(2)}) copy-start(s32[6]{0:T(128)} %constant.128.clone) | copy-start | bytes 76
  24.4 23.4 %collective-permute-start = (f32[256,256]{1,0:T(8,128)}, f32[256,256]{1,0:T(8,128)S(1)}, u32[]{:S(2)}, u32[]{:S(2)}) collective-permute-start(f32[256,256]{1,0:T(8,128)} %slice_bitcast_fusion.7), channel_id=1, source_target_pairs={{0,4},{4,8},{8,12},{12,16},{16,20},{20,24},{24,28},{28,32},{32,36}... | collective-permute-start | bytes 786440 | tf_op jit(solution)/shard_map/ppermute | solution.py:21
  28.5 20.3 %collective-permute-start.1 = (f32[2,256,128]{2,1,0:T(8,128)}, f32[2,256,128]{2,1,0:T(8,128)S(1)}, u32[]{:S(2)}, u32[]{:S(2)}) collective-permute-start(f32[2,256,128]{2,1,0:T(8,128)} %slice.225), channel_id=1, source_target_pairs={{0,1},{1,2},{2,3},{4,5},{5,6},{6,7},{8,9},{9,10},{10,11},{12,13},{... | collective-permute-start | bytes 786440 | tf_op jit(solution)/shard_map/ppermute | solution.py:21
  38.8 10.1 %copy-start.3 = (f32[2,256,256]{2,1,0:T(8,128)S(1)}, f32[2,256,256]{2,1,0:T(8,128)}, u32[]{:S(2)}) copy-start(f32[2,256,256]{2,1,0:T(8,128)} %slice.224) | copy-start | bytes 1572868
  38.8 10.1 %copy-start.4 = (f32[2,256,128]{2,1,0:T(8,128)S(1)}, f32[2,256,128]{2,1,0:T(8,128)}, u32[]{:S(2)}) copy-start(f32[2,256,128]{2,1,0:T(8,128)} %slice.226) | copy-start | bytes 786436
  50.2 1.4 copy-start
  58.9 11.4 %collective-permute-start.2 = (f32[256,256]{1,0:T(8,128)S(1)}, f32[256,256]{1,0:T(8,128)S(1)}, u32[]{:S(2)}, u32[]{:S(2)}) collective-permute-start(f32[256,256]{1,0:T(8,128)S(1)} %get-tuple-element.46), channel_id=1, source_target_pairs={{4,0},{8,4},{12,8},{16,12},{20,16},{24,20},{28,24},{32,28},{36,32}... | collective-permute-start | bytes 786440 | tf_op jit(solution)/shard_map/ppermute | solution.py:21
  63.3 9.2 %collective-permute-start.5 = (f32[2,256,128]{2,1,0:T(8,128)S(1)}, f32[2,256,128]{2,1,0:T(8,128)S(1)}, u32[]{:S(2)}, u32[]{:S(2)}) collective-permute-start(f32[2,256,128]{2,1,0:T(8,128)S(1)} %get-tuple-element.49), channel_id=1, source_target_pairs={{0,1},{1,2},{2,3},{4,5},{5,6},{6,7},{8,9},{9,10},{10,11},{12,13},{... | collective-permute-start | bytes 786440 | tf_op jit(solution)/shard_map/ppermute | solution.py:21
  66.9 9.8 %collective-permute-start.3 = (f32[2,256,128]{2,1,0:T(8,128)S(1)}, f32[2,256,128]{2,1,0:T(8,128)S(1)}, u32[]{:S(2)}, u32[]{:S(2)}) collective-permute-start(f32[2,256,128]{2,1,0:T(8,128)S(1)} %get-tuple-element.50), channel_id=1, source_target_pairs={{1,0},{2,1},{3,2},{5,4},{6,5},{7,6},{9,8},{10,9},{11,10},{13,12},{... | collective-permute-start | bytes 786440 | tf_op jit(solution)/shard_map/ppermute | solution.py:21
  68.2 8.8 %collective-permute-start.4 = (f32[256,256]{1,0:T(8,128)S(1)}, f32[256,256]{1,0:T(8,128)S(1)}, u32[]{:S(2)}, u32[]{:S(2)}) collective-permute-start(f32[256,256]{1,0:T(8,128)S(1)} %get-tuple-element.45), channel_id=1, source_target_pairs={{0,4},{4,8},{8,12},{12,16},{16,20},{20,24},{24,28},{28,32},{32,36}... | collective-permute-start | bytes 786440 | tf_op jit(solution)/shard_map/ppermute | solution.py:21
  77.1 1.7 %copy-start.2 = (bf16[2,768,768]{2,1,0:T(8,128)(2,1)S(1)}, bf16[2,768,768]{2,1,0:T(8,128)(2,1)}, u32[]{:S(2)}) copy-start(bf16[2,768,768]{2,1,0:T(8,128)(2,1)} %shard_map.69) | copy-start | bytes 7077892
  80.5 10.7 %collective-permute-start.6 = (f32[256,256]{1,0:T(8,128)S(1)}, f32[256,256]{1,0:T(8,128)S(1)}, u32[]{:S(2)}, u32[]{:S(2)}) collective-permute-start(f32[256,256]{1,0:T(8,128)S(1)} %get-tuple-element.38), channel_id=1, source_target_pairs={{4,0},{8,4},{12,8},{16,12},{20,16},{24,20},{28,24},{32,28},{36,32}... | collective-permute-start | bytes 786440 | tf_op jit(solution)/shard_map/ppermute | solution.py:21
  83.7 9.4 %collective-permute-start.9 = (f32[2,256,128]{2,1,0:T(8,128)S(1)}, f32[2,256,128]{2,1,0:T(8,128)S(1)}, u32[]{:S(2)}, u32[]{:S(2)}) collective-permute-start(f32[2,256,128]{2,1,0:T(8,128)S(1)} %get-tuple-element.41), channel_id=1, source_target_pairs={{0,1},{1,2},{2,3},{4,5},{5,6},{6,7},{8,9},{9,10},{10,11},{12,13},{... | collective-permute-start | bytes 786440 | tf_op jit(solution)/shard_map/ppermute | solution.py:21
  87.9 9.2 %collective-permute-start.7 = (f32[2,256,128]{2,1,0:T(8,128)S(1)}, f32[2,256,128]{2,1,0:T(8,128)S(1)}, u32[]{:S(2)}, u32[]{:S(2)}) collective-permute-start(f32[2,256,128]{2,1,0:T(8,128)S(1)} %get-tuple-element.42), channel_id=1, source_target_pairs={{1,0},{2,1},{3,2},{5,4},{6,5},{7,6},{9,8},{10,9},{11,10},{13,12},{... | collective-permute-start | bytes 786440 | tf_op jit(solution)/shard_map/ppermute | solution.py:21
  89.2 8.4 %collective-permute-start.8 = (f32[256,256]{1,0:T(8,128)S(1)}, f32[256,256]{1,0:T(8,128)S(1)}, u32[]{:S(2)}, u32[]{:S(2)}) collective-permute-start(f32[256,256]{1,0:T(8,128)S(1)} %get-tuple-element.37), channel_id=1, source_target_pairs={{0,4},{4,8},{8,12},{12,16},{16,20},{20,24},{24,28},{28,32},{32,36}... | collective-permute-start | bytes 786440 | tf_op jit(solution)/shard_map/ppermute | solution.py:21
  99.7 12.0 %collective-permute-start.10 = (f32[256,256]{1,0:T(8,128)S(1)}, f32[256,256]{1,0:T(8,128)S(1)}, u32[]{:S(2)}, u32[]{:S(2)}) collective-permute-start(f32[256,256]{1,0:T(8,128)S(1)} %get-tuple-element.29), channel_id=1, source_target_pairs={{4,0},{8,4},{12,8},{16,12},{20,16},{24,20},{28,24},{32,28},{36,32}... | collective-permute-start | bytes 786440 | tf_op jit(solution)/shard_map/ppermute | solution.py:21
  103.9 9.9 %collective-permute-start.13 = (f32[2,256,128]{2,1,0:T(8,128)S(1)}, f32[2,256,128]{2,1,0:T(8,128)S(1)}, u32[]{:S(2)}, u32[]{:S(2)}) collective-permute-start(f32[2,256,128]{2,1,0:T(8,128)S(1)} %get-tuple-element.33), channel_id=1, source_target_pairs={{0,1},{1,2},{2,3},{4,5},{5,6},{6,7},{8,9},{9,10},{10,11},{12,13},{... | collective-permute-start | bytes 786440 | tf_op jit(solution)/shard_map/ppermute | solution.py:21
  108.2 9.5 %collective-permute-start.11 = (f32[2,256,128]{2,1,0:T(8,128)S(1)}, f32[2,256,128]{2,1,0:T(8,128)S(1)}, u32[]{:S(2)}, u32[]{:S(2)}) collective-permute-start(f32[2,256,128]{2,1,0:T(8,128)S(1)} %get-tuple-element.34), channel_id=1, source_target_pairs={{1,0},{2,1},{3,2},{5,4},{6,5},{7,6},{9,8},{10,9},{11,10},{13,12},{... | collective-permute-start | bytes 786440 | tf_op jit(solution)/shard_map/ppermute | solution.py:21
  109.6 8.7 %collective-permute-start.12 = (f32[256,256]{1,0:T(8,128)S(1)}, f32[256,256]{1,0:T(8,128)S(1)}, u32[]{:S(2)}, u32[]{:S(2)}) collective-permute-start(f32[256,256]{1,0:T(8,128)S(1)} %get-tuple-element.28), channel_id=1, source_target_pairs={{0,4},{4,8},{8,12},{12,16},{16,20},{20,24},{24,28},{28,32},{32,36}... | collective-permute-start | bytes 786440 | tf_op jit(solution)/shard_map/ppermute | solution.py:21
  120.2 7.7 %collective-permute-start.14 = (f32[256,256]{1,0:T(8,128)S(1)}, f32[256,256]{1,0:T(8,128)S(1)}, u32[]{:S(2)}, u32[]{:S(2)}) collective-permute-start(f32[256,256]{1,0:T(8,128)S(1)} %get-tuple-element.25), channel_id=1, source_target_pairs={{4,0},{8,4},{12,8},{16,12},{20,16},{24,20},{28,24},{32,28},{36,32}... | collective-permute-start | bytes 786440 | tf_op jit(solution)/shard_map/ppermute | solution.py:21
  123.7 10.9 %collective-permute-start.15 = (f32[2,256,128]{2,1,0:T(8,128)S(1)}, f32[2,256,128]{2,1,0:T(8,128)S(1)}, u32[]{:S(2)}, u32[]{:S(2)}) collective-permute-start(f32[2,256,128]{2,1,0:T(8,128)S(1)} %slice.266), channel_id=1, source_target_pairs={{1,0},{2,1},{3,2},{5,4},{6,5},{7,6},{9,8},{10,9},{11,10},{13,12},{... | collective-permute-start | bytes 786440 | tf_op jit(solution)/shard_map/ppermute | solution.py:21
  125.0 9.6 %copy-start.1 = (f32[2,1,256,384]{3,2,1,0:T(8,128)S(1)}, f32[2,1,256,384]{3,2,1,0:T(8,128)}, u32[]{:S(2)}) copy-start(f32[2,1,256,384]{3,2,1,0:T(8,128)} %param.8) | copy-start | bytes 2359300
